TPU v7x, 128 devices: a whole 4x4x4 slice. The times are simulated.
128 devices in a mesh: rep: 8 (over z_hi, x), shard: 16 (over y, z_lo, core).
Axes of the slice: x: 4, y: 4, z: 4 (z_hi: 2, z_lo: 2; z = z_hi * 2 + z_lo), core: 2. Of those that a mesh axis runs over, the one named last changes fastest.
Arguments:
- inner_wqkv: float32 [8, 2048, 4096], P('rep', 'shard'), may hold values from -8.5 to 8.5
- inner_w1: float32 [8, 2048, 6144], P('rep', 'shard'), may hold values from -8.5 to 8.5
- inner_w3: float32 [8, 2048, 6144], P('rep', 'shard'), may hold values from -8.5 to 8.5
- inner_wo: float32 [8, 2048, 2048], P('rep', 'shard'), may hold values from -8.5 to 8.5
- inner_w2: float32 [8, 6144, 2048], P('rep', 'shard'), may hold values from -8.5 to 8.5
- outer_wqkv: float32 [2048, 4096], P('shard', 'rep'), may hold values from -8 to 8
- outer_w1: float32 [2048, 6144], P('shard', 'rep'), may hold values from -8 to 8
- outer_w3: float32 [2048, 6144], P('shard', 'rep'), may hold values from -8 to 8
- outer_wo: float32 [2048, 2048], P('shard', 'rep'), may hold values from -8 to 8
- outer_w2: float32 [6144, 2048], P('shard', 'rep'), may hold values from -8 to 8
- moment_wqkv: float32 [2048, 4096], P('shard', 'rep'), may hold values from -0.4 to 0.4
- moment_w1: float32 [2048, 6144], P('shard', 'rep'), may hold values from -0.4 to 0.4
- moment_w3: float32 [2048, 6144], P('shard', 'rep'), may hold values from -0.4 to 0.4
- moment_wo: float32 [2048, 2048], P('shard', 'rep'), may hold values from -0.4 to 0.4
- moment_w2: float32 [6144, 2048], P('shard', 'rep'), may hold values from -0.4 to 0.4
- basis_wo: float32 [2048, 64], P('shard'), may hold values from -0.5 to 0.5
- basis_w2: float32 [6144, 64], P('shard'), may hold values from -0.3125 to 0.3125
Outputs:
- weights_wqkv: bfloat16 [2048, 4096], P('shard')
- weights_w1: bfloat16 [2048, 6144], P('shard')
- weights_w3: bfloat16 [2048, 6144], P('shard')
- weights_wo: bfloat16 [2048, 2048], P('shard')
- weights_w2: bfloat16 [6144, 2048], P('shard')
- master_wqkv: float32 [2048, 4096], P('shard', 'rep')
- master_w1: float32 [2048, 6144], P('shard', 'rep')
- master_w3: float32 [2048, 6144], P('shard', 'rep')
- master_wo: float32 [2048, 2048], P('shard', 'rep')
- master_w2: float32 [6144, 2048], P('shard', 'rep')
- momentum_wqkv: float32 [2048, 4096], P('shard', 'rep')
- momentum_w1: float32 [2048, 6144], P('shard', 'rep')
- momentum_w3: float32 [2048, 6144], P('shard', 'rep')
- momentum_wo: float32 [2048, 2048], P('shard', 'rep')
- momentum_w2: float32 [6144, 2048], P('shard', 'rep')
All inputs are finite; a program needn't handle non-finite values.
Results may differ from a plain program's by a relative error of at most 0.007.
Values may be sent and summed in bfloat16 or wider, within the bound.
No kernel may reach another device: no remote copies, remote signals or barrier semaphores. Data moves between devices by JAX's collectives and lax.ppermute only.
A program may use at most 128 MiB of HBM per device.

v0:
```python
import jax
import jax.numpy as jnp
from jax import lax
from jax.sharding import PartitionSpec as P

rate_outer = 0.7
decay_moment = 0.9


def project(basis, matrix):
    return lax.dot_general(
        basis,
        matrix,
        (((0,), (0,)), ((), ())),
        precision=lax.Precision.HIGHEST,
        preferred_element_type=jnp.float32,
    )


def rebuild(basis, coeff):
    return jnp.dot(
        basis, coeff, precision=lax.Precision.HIGHEST, preferred_element_type=jnp.float32
    )


def nesterov(outer, moment, delta):
    moment_new = decay_moment * moment + delta
    master = outer - rate_outer * (delta + decay_moment * moment_new)
    return (master.astype(jnp.bfloat16), master, moment_new)


def on_device(
    inner_wqkv,
    inner_w1,
    inner_w3,
    inner_wo,
    inner_w2,
    outer_wqkv,
    outer_w1,
    outer_w3,
    outer_wo,
    outer_w2,
    moment_wqkv,
    moment_w1,
    moment_w3,
    moment_wo,
    moment_w2,
    basis_wo,
    basis_w2,
):
    groups = lax.axis_size("rep")
    width = outer_wo.shape[1]
    start = lax.axis_index("rep") * width
    summed = (
        lax.psum_scatter(inner_wqkv[0], "rep", scatter_dimension=1, tiled=True),
        lax.psum_scatter(inner_w1[0], "rep", scatter_dimension=1, tiled=True),
        lax.psum_scatter(inner_w3[0], "rep", scatter_dimension=1, tiled=True),
    )
    d_qkv = outer_wqkv - summed[0] / groups
    d_one = outer_w1 - summed[1] / groups
    d_three = outer_w3 - summed[2] / groups
    pairs = ((inner_wo[0], outer_wo, basis_wo), (inner_w2[0], outer_w2, basis_w2))
    terms = []
    for inner_part, outer_part, basis in pairs:
        whole_proj = -project(basis, inner_part) / groups
        owned = project(basis, outer_part) + lax.dynamic_slice_in_dim(whole_proj, start, width, 1)
        terms.append(lax.dynamic_update_slice_in_dim(whole_proj, owned, start, 1))
    totals = lax.psum((terms[0], terms[1]), ("rep", "shard"))
    coeff_out = lax.dynamic_slice_in_dim(totals[0], start, width, 1)
    coeff_down = lax.dynamic_slice_in_dim(totals[1], start, width, 1)
    d_out = rebuild(basis_wo, coeff_out)
    d_down = rebuild(basis_w2, coeff_down)
    a0, b0, c0 = nesterov(outer_wqkv, moment_wqkv, d_qkv)
    a1, b1, c1 = nesterov(outer_w1, moment_w1, d_one)
    a3, b3, c3 = nesterov(outer_w3, moment_w3, d_three)
    ao, bo, co = nesterov(outer_wo, moment_wo, d_out)
    a2, b2, c2 = nesterov(outer_w2, moment_w2, d_down)
    fresh = (
        lax.all_gather(a0, "rep", axis=1, tiled=True),
        lax.all_gather(a1, "rep", axis=1, tiled=True),
        lax.all_gather(a3, "rep", axis=1, tiled=True),
        lax.all_gather(ao, "rep", axis=1, tiled=True),
        lax.all_gather(a2, "rep", axis=1, tiled=True),
    )
    return (
        fresh[0],
        fresh[1],
        fresh[2],
        fresh[3],
        fresh[4],
        b0,
        b1,
        b3,
        bo,
        b2,
        c0,
        c1,
        c3,
        co,
        c2,
    )


def solution(mesh):
    return jax.shard_map(
        on_device,
        mesh=mesh,
        in_specs=(
            P("rep", "shard", None),
            P("rep", "shard", None),
            P("rep", "shard", None),
            P("rep", "shard", None),
            P("rep", "shard", None),
            P("shard", "rep"),
            P("shard", "rep"),
            P("shard", "rep"),
            P("shard", "rep"),
            P("shard", "rep"),
            P("shard", "rep"),
            P("shard", "rep"),
            P("shard", "rep"),
            P("shard", "rep"),
            P("shard", "rep"),
            P("shard", None),
            P("shard", None),
        ),
        out_specs=(
            P("shard", None),
            P("shard", None),
            P("shard", None),
            P("shard", None),
            P("shard", None),
            P("shard", "rep"),
            P("shard", "rep"),
            P("shard", "rep"),
            P("shard", "rep"),
            P("shard", "rep"),
            P("shard", "rep"),
            P("shard", "rep"),
            P("shard", "rep"),
            P("shard", "rep"),
            P("shard", "rep"),
        ),
        check_vma=False,
    )
```

profile of v0, /device:TPU:6, one launch (start us, length us, event | category | flops | bytes accessed | tf_op | source)
XLA Modules:
  0.0 489.7 jit_solution(644622972278131789)
XLA Ops:
  8.1 1.8 copy-done
  9.9 3.8 fusion.5
  13.7 1.5 fusion.8
  15.2 1.8 fusion.10
  17.0 1.7 fusion.9
  20.5 0.9 copy.35
  21.5 1.9 copy.34
  23.4 149.8 %all-reduce.3.cloned.1.call-done = (f32[64,2048]{1,0:T(8,128)}, f32[64,2048]{1,0:T(8,128)}) async-done(((f32[64,2048]{1,0:T(8,128)}, f32[64,2048]{1,0:T(8,128)}), (f32[64,2048]{1,0:T(8,128)}, f32[64,2048]{1,0:T(8,128)})) %all-reduce.3.cloned.1.call-update) | async-done | bytes 1048592 | tf_op jit(solution)/shard_map/psum | solution.py:68
  173.1 2.6 fusion.16
  175.8 2.0 fusion.20
  177.9 7.5 %reduce-scatter.6.cloned.1.call-done = f32[128,768]{1,0:T(8,128)} async-done(((f32[128,6144]{1,0:T(8,128)}), f32[128,768]{1,0:T(8,128)}) %reduce-scatter.6.cloned.1.call-update) | async-done | bytes 393232 | tf_op jit(solution)/shard_map/reduce_scatter | solution.py:56
  185.4 2.3 fusion.19
  187.8 81.1 %reduce-scatter.8.cloned.1.call-done = f32[128,768]{1,0:T(8,128)} async-done(((f32[128,6144]{1,0:T(8,128)}), f32[128,768]{1,0:T(8,128)}) %reduce-scatter.8.cloned.1.call-update) | async-done | bytes 393232 | tf_op jit(solution)/shard_map/reduce_scatter | solution.py:57
  268.9 2.3 fusion.18
  271.2 1.7 copy.33
  272.9 1.7 copy.32
  274.5 1.9 copy.39
  276.4 0.9 copy.41
  277.3 1.4 fusion.17
  278.8 37.2 %all_gather.18 = bf16[128,2048]{0,1:T(8,128)(2,1)} all-gather(bf16[128,256]{0,1:T(8,128)(2,1)S(1)} %get-tuple-element.34), channel_id=1, replica_groups=mesh['rep'=8,'shard'=16] {'rep'}, dimensions={1}, use_global_device_ids=true | all-gather | bytes 589824 | tf_op jit(solution)/shard_map/all_gather | solution.py:82
  316.0 2.0 copy.36
  318.0 0.8 copy.38
  318.8 0.8 copy.40
  319.5 3.5 all-gather.11.cloned.1.call-done
  323.0 2.6 copy.37
  325.6 46.8 %all-gather.5.cloned.1.call-done = bf16[128,4096]{1,0:T(8,128)(2,1)} async-done(((bf16[128,512]{1,0:T(8,128)(2,1)}), bf16[128,4096]{1,0:T(8,128)(2,1)}) %all-gather.5.cloned.1.call-update) | async-done | bytes 1048592 | tf_op jit(solution)/shard_map/all_gather | solution.py:79
  372.5 52.2 %all-gather.7.cloned.1.call-done = bf16[128,6144]{1,0:T(8,128)(2,1)} async-done(((bf16[128,768]{1,0:T(8,128)(2,1)}), bf16[128,6144]{1,0:T(8,128)(2,1)}) %all-gather.7.cloned.1.call-update) | async-done | bytes 1572880 | tf_op jit(solution)/shard_map/all_gather | solution.py:80
  424.7 52.1 %all-gather.9.cloned.1.call-done = bf16[128,6144]{1,0:T(8,128)(2,1)} async-done(((bf16[128,768]{1,0:T(8,128)(2,1)}), bf16[128,6144]{1,0:T(8,128)(2,1)}) %all-gather.9.cloned.1.call-update) | async-done | bytes 1572880 | tf_op jit(solution)/shard_map/all_gather | solution.py:81
  476.7 2.4 copy.49
  479.2 1.1 copy.50
  480.3 0.8 copy-done.2
  481.1 1.1 copy.51
  (31 shorter events, 2.0 us)
Async XLA Ops:
  8.0 1.9 copy-start
  8.0 165.1 %all-reduce.3.cloned.1.call-start = ((), (), s32[]{:S(2)}) async-start(), calls=%async_computation.10 | async-start | bytes 2097152 | tf_op jit(solution)/shard_map/psum | solution.py:68
  9.9 3.8 copy-start.4
  9.9 3.8 copy-start.7
  9.9 5.3 %copy-start.3 = (f32[384,256]{1,0:T(8,128)S(1)}, f32[384,256]{1,0:T(8,128)}, u32[]{:S(2)}) copy-start(f32[384,256]{1,0:T(8,128)} %param.26) | copy-start | bytes 1179652
  9.9 5.3 %copy-start.5 = (f32[384,64]{0,1:T(8,128)S(1)}, f32[384,64]{0,1:T(8,128)}, u32[]{:S(2)}) copy-start(f32[384,64]{0,1:T(8,128)} %param.33) | copy-start | bytes 294916
  9.9 7.1 %copy-start.6 = (f32[128,256]{1,0:T(8,128)S(1)}, f32[128,256]{1,0:T(8,128)}, u32[]{:S(2)}) copy-start(f32[128,256]{1,0:T(8,128)} %param.25) | copy-start | bytes 393220
  18.7 157.1 %reduce-scatter.4.cloned.1.call-start = ((), (), s32[]{:S(2)}) async-start(), calls=%async_computation.3 | async-start | bytes 2359296 | tf_op jit(solution)/shard_map/reduce_scatter | solution.py:55
  19.3 166.1 %reduce-scatter.6.cloned.1.call-start = ((), (), s32[]{:S(2)}) async-start(), calls=%async_computation.5 | async-start | bytes 3538944 | tf_op jit(solution)/shard_map/reduce_scatter | solution.py:56
  19.9 249.0 %reduce-scatter.8.cloned.1.call-start = ((), (), s32[]{:S(2)}) async-start(), calls=%async_computation.7 | async-start | bytes 3538944 | tf_op jit(solution)/shard_map/reduce_scatter | solution.py:57
  20.5 302.5 %all-gather.11.cloned.1.call-start = ((), (), s32[]{:S(2)}) async-start(), calls=%async_computation.9 | async-start | bytes 1769472 | tf_op jit(solution)/shard_map/all_gather | solution.py:83
  175.8 196.7 %all-gather.5.cloned.1.call-start = ((), (), s32[]{:S(2)}) async-start(), calls=%async_computation.4 | async-start | bytes 1179648 | tf_op jit(solution)/shard_map/all_gather | solution.py:79
  177.9 246.8 %all-gather.7.cloned.1.call-start = ((), (), s32[]{:S(2)}) async-start(), calls=%async_computation.6 | async-start | bytes 1769472 | tf_op jit(solution)/shard_map/all_gather | solution.py:80
  187.7 289.0 %all-gather.9.cloned.1.call-start = ((), (), s32[]{:S(2)}) async-start(), calls=%async_computation.8 | async-start | bytes 1769472 | tf_op jit(solution)/shard_map/all_gather | solution.py:81
  476.7 2.4 copy-start.1
  479.2 2.0 copy-start.2
Sparse Core Ops, SparseCore 0:
  18.9 154.2 all-reduce.2
Sparse Core Ops, SparseCore 1:
  23.0 78.7 reduce-scatter.3
  105.5 79.9 reduce-scatter.5
  189.2 79.6 reduce-scatter.7
  271.8 51.2 all-gather.10
  325.8 46.6 all-gather.4
  375.3 49.3 all-gather.6
  427.4 49.3 all-gather.8
where the time goes:
time: 491 us; the launch traced here: 490 us
  waiting for transfers between devices  395 us (80%)
  blocking collectives  37.2 us (8%)
  local copies, waits for them, and re-layouts  22.5 us (5%)
  between operations  15.6 us (3%)
  matrix products  12.8 us (3%)
  other arithmetic  6.58 us (1%)
    psum x1, waiting for transfers between devices, on_device(): totals = lax.psum((terms[0], terms[1]), ('rep', 'shard'))  150 us
    reduce_scatter x1, waiting for transfers between devices, on_device(): lax.psum_scatter(inner_w3[0], 'rep', scatter_dimension=1, tiled=True)  81.1 us
    all_gather x1, waiting for transfers between devices, on_device(): lax.all_gather(a1, 'rep', axis=1, tiled=True)  52.2 us
    all_gather x1, waiting for transfers between devices, on_device(): lax.all_gather(a3, 'rep', axis=1, tiled=True)  52.1 us
    all_gather x1, waiting for transfers between devices, on_device(): lax.all_gather(a0, 'rep', axis=1, tiled=True)  46.8 us
    all_gather x1, blocking collectives, on_device(): lax.all_gather(ao, 'rep', axis=1, tiled=True)  37.2 us
    unnamed x29, local copies, waits for them, and re-layouts  22.5 us
  transfers between devices with their start and end apart: 8, of which 7 were waited for; matrix products, arithmetic and copies ran while one was open for 5% of the time, Pallas kernels for 0%

commit v1 on v0

--- a/solution.py
+++ b/solution.py
@@ -29,6 +29,20 @@
     return (master.astype(jnp.bfloat16), master, moment_new)
 
 
+def by_owner(a, n):
+    r, c = a.shape
+    return a.reshape(r, n, c // n).transpose(1, 0, 2)
+
+
+def from_owners(g):
+    n, r, w = g.shape
+    return g.transpose(1, 0, 2).reshape(r, n * w)
+
+
+def gather_rep(y, n):
+    return lax.all_to_all(jnp.broadcast_to(y[None], (n,) + y.shape), "rep", 0, 0, tiled=True)
+
+
 def on_device(
     inner_wqkv,
     inner_w1,
@@ -48,46 +62,54 @@
     basis_wo,
     basis_w2,
 ):
-    groups = lax.axis_size("rep")
-    width = outer_wo.shape[1]
-    start = lax.axis_index("rep") * width
-    summed = (
-        lax.psum_scatter(inner_wqkv[0], "rep", scatter_dimension=1, tiled=True),
-        lax.psum_scatter(inner_w1[0], "rep", scatter_dimension=1, tiled=True),
-        lax.psum_scatter(inner_w3[0], "rep", scatter_dimension=1, tiled=True),
+    n = lax.axis_size("rep")
+    w_qkv = outer_wqkv.shape[1]
+    w_ff = outer_w1.shape[1]
+    w_o = outer_wo.shape[1]
+    w_2 = outer_w2.shape[1]
+    rows = inner_wqkv.shape[1]
+    rank = basis_wo.shape[1]
+    width = w_qkv + 2 * w_ff
+
+    coef_part = jnp.concatenate(
+        [by_owner(project(basis_wo, inner_wo[0]), n), by_owner(project(basis_w2, inner_w2[0]), n)],
+        axis=2,
     )
-    d_qkv = outer_wqkv - summed[0] / groups
-    d_one = outer_w1 - summed[1] / groups
-    d_three = outer_w3 - summed[2] / groups
-    pairs = ((inner_wo[0], outer_wo, basis_wo), (inner_w2[0], outer_w2, basis_w2))
-    terms = []
-    for inner_part, outer_part, basis in pairs:
-        whole_proj = -project(basis, inner_part) / groups
-        owned = project(basis, outer_part) + lax.dynamic_slice_in_dim(whole_proj, start, width, 1)
-        terms.append(lax.dynamic_update_slice_in_dim(whole_proj, owned, start, 1))
-    totals = lax.psum((terms[0], terms[1]), ("rep", "shard"))
-    coeff_out = lax.dynamic_slice_in_dim(totals[0], start, width, 1)
-    coeff_down = lax.dynamic_slice_in_dim(totals[1], start, width, 1)
-    d_out = rebuild(basis_wo, coeff_out)
-    d_down = rebuild(basis_w2, coeff_down)
+    dense = jnp.concatenate(
+        [by_owner(inner_wqkv[0], n), by_owner(inner_w1[0], n), by_owner(inner_w3[0], n)], axis=2
+    )
+    send = jnp.concatenate([dense, coef_part.reshape(n, -1, width)], axis=1)
+    total = jnp.sum(lax.all_to_all(send, "rep", 0, 0, tiled=True), axis=0)
+
+    summed = total[:rows]
+    own = jnp.concatenate([project(basis_wo, outer_wo), project(basis_w2, outer_w2)], axis=1)
+    coeff = lax.psum(own - total[rows:].reshape(rank, w_o + w_2) / n, "shard")
+
+    d_qkv = outer_wqkv - summed[:, :w_qkv] / n
+    d_one = outer_w1 - summed[:, w_qkv : w_qkv + w_ff] / n
+    d_three = outer_w3 - summed[:, w_qkv + w_ff :] / n
     a0, b0, c0 = nesterov(outer_wqkv, moment_wqkv, d_qkv)
     a1, b1, c1 = nesterov(outer_w1, moment_w1, d_one)
     a3, b3, c3 = nesterov(outer_w3, moment_w3, d_three)
+    dense_w = gather_rep(jnp.concatenate([a0, a1, a3], axis=1), n)
+
+    d_out = rebuild(basis_wo, coeff[:, :w_o])
+    d_down = rebuild(basis_w2, coeff[:, w_o:])
     ao, bo, co = nesterov(outer_wo, moment_wo, d_out)
     a2, b2, c2 = nesterov(outer_w2, moment_w2, d_down)
-    fresh = (
-        lax.all_gather(a0, "rep", axis=1, tiled=True),
-        lax.all_gather(a1, "rep", axis=1, tiled=True),
-        lax.all_gather(a3, "rep", axis=1, tiled=True),
-        lax.all_gather(ao, "rep", axis=1, tiled=True),
-        lax.all_gather(a2, "rep", axis=1, tiled=True),
-    )
+    low_w = gather_rep(jnp.concatenate([ao, a2.reshape(rows, -1)], axis=1), n)
+
+    weights_wqkv = from_owners(dense_w[:, :, :w_qkv])
+    weights_w1 = from_owners(dense_w[:, :, w_qkv : w_qkv + w_ff])
+    weights_w3 = from_owners(dense_w[:, :, w_qkv + w_ff :])
+    weights_wo = from_owners(low_w[:, :, :w_o])
+    weights_w2 = from_owners(low_w[:, :, w_o:].reshape(n, -1, w_2))
     return (
-        fresh[0],
-        fresh[1],
-        fresh[2],
-        fresh[3],
-        fresh[4],
+        weights_wqkv,
+        weights_w1,
+        weights_w3,
+        weights_wo,
+        weights_w2,
         b0,
         b1,
         b3,

time: 491 us -> 457 us (0.931)
  waiting for transfers between devices: 395 us -> 325 us
  local copies, waits for them, and re-layouts: 22.5 us -> 63.8 us
  blocking collectives: 37.2 us -> 0 us
  starting transfers between devices: 0.34 us -> 22.4 us
  other arithmetic: 6.58 us -> 20.6 us
    all_to_all x0 -> x3, waiting for transfers between devices: none -> 207 us  [the longest x1 139 us: on_device(): total = jnp.sum(lax.all_to_all(send, 'rep', 0, 0, tiled=True), axis=0)]
    all_gather x4 -> x0, waiting for transfers between devices: 155 us -> none  [the longest x1 52.2 us: on_device(): lax.all_gather(a1, 'rep', axis=1, tiled=True)]
    reduce_scatter x3 -> x0, waiting for transfers between devices: 88.6 us -> none  [the longest x1 81.1 us: on_device(): lax.psum_scatter(inner_w3[0], 'rep', scatter_dimension=1, tiled=True)]
    all_gather x1 -> x0, blocking collectives: 37.2 us -> none  [on_device(): lax.all_gather(ao, 'rep', axis=1, tiled=True)]
    psum x1, waiting for transfers between devices: 150 us -> 118 us  [on_device(): coeff = lax.psum(own - total[rows:].reshape(rank, w_o + w_2) / n, 'shard')]
    all_to_all x0 -> x3, starting transfers between devices: none -> 22.4 us  [the longest x2 14.2 us: gather_rep(): lax.all_to_all(jnp.broadcast_to(y[None], (n,) + y.shape), 'rep', 0, 0, ti...]
    concatenate x0 -> x1, local copies, waits for them, and re-layouts: none -> 14.7 us  [on_device(): send = jnp.concatenate([dense, coef_part.reshape(n, -1, width)], axis=1)]
    reshape x0 -> x5, local copies, waits for them, and re-layouts: none -> 11.7 us  [the longest x2 5.09 us: on_device(): send = jnp.concatenate([dense, coef_part.reshape(n, -1, width)], axis=1)]
  transfers between devices with their start and end apart: 8 -> 4, of which waited for: 7 -> 4; matrix products, arithmetic and copies ran while one was open for 5% -> 4% of each run, Pallas kernels for 0% -> 0%
where the time goes in v1:
time: 457 us; the launch traced here: 455 us
  waiting for transfers between devices  325 us (71%)
  local copies, waits for them, and re-layouts  63.8 us (14%)
  starting transfers between devices  22.4 us (5%)
  other arithmetic  20.6 us (5%)
  between operations  14.3 us (3%)
  matrix products  9.19 us (2%)
    all_to_all x1, waiting for transfers between devices, on_device(): total = jnp.sum(lax.all_to_all(send, 'rep', 0, 0, tiled=True), axis=0)  139 us
    psum x1, waiting for transfers between devices, on_device(): coeff = lax.psum(own - total[rows:].reshape(rank, w_o + w_2) / n, 'shard')  118 us
    all_to_all x2, waiting for transfers between devices, gather_rep(): lax.all_to_all(jnp.broadcast_to(y[None], (n,) + y.shape), 'rep', 0, 0, ti...  67.3 us
    unnamed x39, local copies, waits for them, and re-layouts  22.1 us
    concatenate x1, local copies, waits for them, and re-layouts, on_device(): send = jnp.concatenate([dense, coef_part.reshape(n, -1, width)], axis=1)  14.7 us
    all_to_all x2, starting transfers between devices, gather_rep(): lax.all_to_all(jnp.broadcast_to(y[None], (n,) + y.shape), 'rep', 0, 0, ti...  14.2 us
    concatenate x1, other arithmetic, on_device(): send = jnp.concatenate([dense, coef_part.reshape(n, -1, width)], axis=1)  10.6 us
  transfers between devices with their start and end apart: 4, of which 4 were waited for; matrix products, arithmetic and copies ran while one was open for 4% of the time, Pallas kernels for 0%

profile of v1, /device:TPU:6, one launch (start us, length us, event | category | flops | bytes accessed | tf_op | source)
XLA Modules:
  0.0 455.1 jit_solution(16131179294469617486)
XLA Ops:
  7.2 2.4 copy.97
  9.6 2.5 copy.96
  12.2 3.2 convolution_bitcast_fusion
  17.3 4.6 %copy.75 = f32[8,16,2048]{1,2,0:T(8,128)} copy(f32[8,16,2048]{2,1,0:T(8,128)S(1)} %reshape.63) | data formatting | bytes 2097152 | tf_op jit(solution)/shard_map/reshape | solution.py:81
  21.9 2.4 copy.71
  24.3 3.6 copy.72
  27.9 3.0 copy.70
  30.9 10.6 %pad_maximum_fusion = f32[8,144,2048]{1,2,0:T(8,128)} fusion(f32[8,16,2048]{1,2,0:T(8,128)} %copy.75, f32[8,128,768]{1,2,0:T(8,128)} %bitcast.55, f32[8,128,768]{1,2,0:T(8,128)S(1)} %bitcast.54, f32[8,128,512]{1,2,0:T(8,128)} %bitcast.57), kind=kLoop, calls=%fused_computation | loop fusion | flops 7077888 | bytes 18874368 | tf_op jit(solution)/shard_map/concatenate | solution.py:81
  41.4 14.7 %copy.76 = f32[8,144,2048]{2,1,0:T(8,128)} copy(f32[8,144,2048]{1,2,0:T(8,128)} %pad_maximum_fusion) | data formatting | bytes 18874368 | tf_op jit(solution)/shard_map/concatenate | solution.py:81
  56.2 8.2 %all-to-all-start = ((f32[8,144,2048]{2,1,0:T(8,128)}), f32[8,144,2048]{2,1,0:T(8,128)}, u32[]{:S(2)}, u32[]{:S(2)}) async-start(f32[8,144,2048]{2,1,0:T(8,128)} %copy.76), calls=%async_computation | async-start | bytes 18874368 | tf_op jit(solution)/shard_map/all_to_all | solution.py:82
  65.0 139.2 %all-to-all-done = f32[8,144,2048]{2,1,0:T(8,128)} async-done(((f32[8,144,2048]{2,1,0:T(8,128)}), f32[8,144,2048]{2,1,0:T(8,128)}, u32[]{:S(2)}, u32[]{:S(2)}) %all-to-all-start) | async-done | bytes 9437216 | tf_op jit(solution)/shard_map/all_to_all | solution.py:82
  204.2 4.7 %reduce_sum.9 = f32[144,2048]{1,0:T(8,128)S(1)} reduce(f32[8,144,2048]{2,1,0:T(8,128)} %all-to-all-done, f32[]{:T(128)} %constant.4.clone.1), dimensions={0}, to_apply=%region_0.0 | reduce | flops 2064384 | bytes 10616836 | tf_op jit(solution)/shard_map/reduce_sum | solution.py:82
  210.2 118.2 %all-reduce.2.cloned.1.call-done = f32[64,512]{1,0:T(8,128)} async-done(((f32[64,512]{1,0:T(8,128)}), f32[64,512]{1,0:T(8,128)}) %all-reduce.2.cloned.1.call-update) | async-done | bytes 131088 | tf_op jit(solution)/shard_map/psum | solution.py:86
  328.4 2.3 fusion.8
  331.0 1.9 fusion.7
  333.0 1.6 broadcast_in_dim.5
  334.6 7.2 %all-to-all-start.2 = ((bf16[8,128,1024]{2,1,0:T(8,128)(2,1)}), bf16[8,128,1024]{2,1,0:T(8,128)(2,1)S(1)}, u32[]{:S(2)}, u32[]{:S(2)}) async-start(bf16[8,128,1024]{2,1,0:T(8,128)(2,1)} %broadcast_in_dim.5), calls=%async_computation.2 | async-start | bytes 4194304 | tf_op jit(solution)/shard_map/all_to_all | solution.py:43
  341.8 1.9 fusion.9
  343.7 2.6 fusion.10
  346.3 23.2 %all-to-all-done.2 = bf16[8,128,1024]{2,1,0:T(8,128)(2,1)S(1)} async-done(((bf16[8,128,1024]{2,1,0:T(8,128)(2,1)}), bf16[8,128,1024]{2,1,0:T(8,128)(2,1)S(1)}, u32[]{:S(2)}, u32[]{:S(2)}) %all-to-all-start.2) | async-done | bytes 2097184 | tf_op jit(solution)/shard_map/all_to_all | solution.py:43
  369.5 2.5 broadcast_in_dim.4
  372.1 7.0 %all-to-all-start.1 = ((bf16[8,128,2048]{2,1,0:T(8,128)(2,1)}), bf16[8,128,2048]{2,1,0:T(8,128)(2,1)}, u32[]{:S(2)}, u32[]{:S(2)}) async-start(bf16[8,128,2048]{2,1,0:T(8,128)(2,1)} %broadcast_in_dim.4), calls=%async_computation.1 | async-start | bytes 8388608 | tf_op jit(solution)/shard_map/all_to_all | solution.py:43
  382.5 1.3 slice.58
  383.8 3.7 reshape.69
  387.5 2.8 copy.102
  391.6 44.1 %all-to-all-done.1 = bf16[8,128,2048]{2,1,0:T(8,128)(2,1)} async-done(((bf16[8,128,2048]{2,1,0:T(8,128)(2,1)}), bf16[8,128,2048]{2,1,0:T(8,128)(2,1)}, u32[]{:S(2)}, u32[]{:S(2)}) %all-to-all-start.1) | async-done | bytes 4194336 | tf_op jit(solution)/shard_map/all_to_all | solution.py:43
  435.7 3.3 fusion.12
  439.0 1.9 copy.99
  440.9 1.6 copy.89
  443.4 1.6 copy.90
  445.0 1.3 slice.51
  447.0 1.3 copy.88
  (48 shorter events, 10.3 us)
Async XLA Ops:
  7.2 5.0 %copy-start = (f32[384,64]{0,1:T(8,128)S(1)}, f32[384,64]{0,1:T(8,128)}, u32[]{:S(2)}) copy-start(f32[384,64]{0,1:T(8,128)} %param.33) | copy-start | bytes 294916
  9.6 5.8 %copy-start.8 = (f32[128,64]{0,1:T(8,128)S(1)}, f32[128,64]{0,1:T(8,128)}, u32[]{:S(2)}) copy-start(f32[128,64]{0,1:T(8,128)} %param.32) | copy-start | bytes 98308
  12.2 3.2 copy-start.1
  56.2 8.2 %copy-start.5 = (f32[128,256]{1,0:T(8,128)S(1)}, f32[128,256]{1,0:T(8,128)}, u32[]{:S(2)}) copy-start(f32[128,256]{1,0:T(8,128)} %param.25) | copy-start | bytes 393220
  56.2 8.4 %copy-start.2 = (f32[384,256]{1,0:T(8,128)S(1)}, f32[384,256]{1,0:T(8,128)}, u32[]{:S(2)}) copy-start(f32[384,256]{1,0:T(8,128)} %param.26) | copy-start | bytes 1179652
  56.2 148.0 %all-to-all-start = ((f32[8,144,2048]{2,1,0:T(8,128)}), f32[8,144,2048]{2,1,0:T(8,128)}, u32[]{:S(2)}, u32[]{:S(2)}) async-start(f32[8,144,2048]{2,1,0:T(8,128)} %copy.76), calls=%async_computation | async-start | bytes 18874368 | tf_op jit(solution)/shard_map/all_to_all | solution.py:82
  64.4 264.0 %all-reduce.2.cloned.1.call-start = ((), (), s32[]{:S(2)}) async-start(), calls=%async_computation.3 | async-start | bytes 262144 | tf_op jit(solution)/shard_map/psum | solution.py:86
  65.0 145.0 %copy-start.7 = (f32[384,256]{1,0:T(8,128)S(1)}, f32[384,256]{1,0:T(8,128)}, u32[]{:S(2)}) copy-start(f32[384,256]{1,0:T(8,128)} %param.31) | copy-start | bytes 1179652
  65.0 145.1 %copy-start.9 = (f32[128,256]{1,0:T(8,128)S(1)}, f32[128,256]{1,0:T(8,128)}, u32[]{:S(2)}) copy-start(f32[128,256]{1,0:T(8,128)} %param.30) | copy-start | bytes 393220
  334.6 34.9 %all-to-all-start.2 = ((bf16[8,128,1024]{2,1,0:T(8,128)(2,1)}), bf16[8,128,1024]{2,1,0:T(8,128)(2,1)S(1)}, u32[]{:S(2)}, u32[]{:S(2)}) async-start(bf16[8,128,1024]{2,1,0:T(8,128)(2,1)} %broadcast_in_dim.5), calls=%async_computation.2 | async-start | bytes 4194304 | tf_op jit(solution)/shard_map/all_to_all | solution.py:43
  372.1 7.1 %copy-start.4 = (f32[384,256]{0,1:T(8,128)S(1)}, f32[384,256]{0,1:T(8,128)}, u32[]{:S(2)}) copy-start(f32[384,256]{0,1:T(8,128)} %get-tuple-element.78) | copy-start | bytes 1179652
  372.1 8.0 %copy-start.3 = (f32[384,256]{0,1:T(8,128)S(1)}, f32[384,256]{0,1:T(8,128)}, u32[]{:S(2)}) copy-start(f32[384,256]{0,1:T(8,128)} %get-tuple-element.93) | copy-start | bytes 1179652
  372.1 8.9 %copy-start.6 = (f32[128,256]{0,1:T(8,128)S(1)}, f32[128,256]{0,1:T(8,128)}, u32[]{:S(2)}) copy-start(f32[128,256]{0,1:T(8,128)} %get-tuple-element.76) | copy-start | bytes 393220
  372.1 63.6 %all-to-all-start.1 = ((bf16[8,128,2048]{2,1,0:T(8,128)(2,1)}), bf16[8,128,2048]{2,1,0:T(8,128)(2,1)}, u32[]{:S(2)}, u32[]{:S(2)}) async-start(bf16[8,128,2048]{2,1,0:T(8,128)(2,1)} %broadcast_in_dim.4), calls=%async_computation.1 | async-start | bytes 8388608 | tf_op jit(solution)/shard_map/all_to_all | solution.py:43
Sparse Core Ops, SparseCore 0:
  209.8 118.5 all-reduce.1

commit v2 on v1

--- a/solution.py
+++ b/solution.py
@@ -29,18 +29,13 @@
     return (master.astype(jnp.bfloat16), master, moment_new)
 
 
-def by_owner(a, n):
-    r, c = a.shape
-    return a.reshape(r, n, c // n).transpose(1, 0, 2)
+def owner_blocks(a, n):
+    w = a.shape[1] // n
+    return [a[:, j * w : (j + 1) * w] for j in range(n)]
 
 
-def from_owners(g):
-    n, r, w = g.shape
-    return g.transpose(1, 0, 2).reshape(r, n * w)
-
-
-def gather_rep(y, n):
-    return lax.all_to_all(jnp.broadcast_to(y[None], (n,) + y.shape), "rep", 0, 0, tiled=True)
+def gather_all(y, axis_name, n):
+    return lax.all_to_all(jnp.broadcast_to(y[None], (n,) + y.shape), axis_name, 0, 0, tiled=True)
 
 
 def on_device(
@@ -63,27 +58,37 @@
     basis_w2,
 ):
     n = lax.axis_size("rep")
+    n_shard = lax.axis_size("shard")
     w_qkv = outer_wqkv.shape[1]
     w_ff = outer_w1.shape[1]
     w_o = outer_wo.shape[1]
     w_2 = outer_w2.shape[1]
     rows = inner_wqkv.shape[1]
+    rows_2 = outer_w2.shape[0]
     rank = basis_wo.shape[1]
     width = w_qkv + 2 * w_ff
+    w_c = w_o + w_2
+    k_c = width // w_c
+    r_c = rank // k_c
 
-    coef_part = jnp.concatenate(
-        [by_owner(project(basis_wo, inner_wo[0]), n), by_owner(project(basis_w2, inner_w2[0]), n)],
-        axis=2,
-    )
-    dense = jnp.concatenate(
-        [by_owner(inner_wqkv[0], n), by_owner(inner_w1[0], n), by_owner(inner_w3[0], n)], axis=2
-    )
-    send = jnp.concatenate([dense, coef_part.reshape(n, -1, width)], axis=1)
-    total = jnp.sum(lax.all_to_all(send, "rep", 0, 0, tiled=True), axis=0)
+    qkv_b = owner_blocks(inner_wqkv[0], n)
+    one_b = owner_blocks(inner_w1[0], n)
+    three_b = owner_blocks(inner_w3[0], n)
+    po_b = owner_blocks(project(basis_wo, inner_wo[0]), n)
+    p2_b = owner_blocks(project(basis_w2, inner_w2[0]), n)
+    send = []
+    for j in range(n):
+        part = jnp.concatenate([po_b[j], p2_b[j]], axis=1)
+        folded = jnp.concatenate([part[k * r_c : (k + 1) * r_c] for k in range(k_c)], axis=1)
+        dense = jnp.concatenate([qkv_b[j], one_b[j], three_b[j]], axis=1)
+        send.append(jnp.concatenate([dense, folded], axis=0))
+    total = jnp.sum(lax.all_to_all(jnp.stack(send), "rep", 0, 0, tiled=True), axis=0)
 
     summed = total[:rows]
+    folded = total[rows:]
+    part = jnp.concatenate([folded[:, k * w_c : (k + 1) * w_c] for k in range(k_c)], axis=0)
     own = jnp.concatenate([project(basis_wo, outer_wo), project(basis_w2, outer_w2)], axis=1)
-    coeff = lax.psum(own - total[rows:].reshape(rank, w_o + w_2) / n, "shard")
+    coeff = jnp.sum(gather_all(own - part / n, "shard", n_shard), axis=0)
 
     d_qkv = outer_wqkv - summed[:, :w_qkv] / n
     d_one = outer_w1 - summed[:, w_qkv : w_qkv + w_ff] / n
@@ -91,19 +96,33 @@
     a0, b0, c0 = nesterov(outer_wqkv, moment_wqkv, d_qkv)
     a1, b1, c1 = nesterov(outer_w1, moment_w1, d_one)
     a3, b3, c3 = nesterov(outer_w3, moment_w3, d_three)
-    dense_w = gather_rep(jnp.concatenate([a0, a1, a3], axis=1), n)
-
     d_out = rebuild(basis_wo, coeff[:, :w_o])
     d_down = rebuild(basis_w2, coeff[:, w_o:])
     ao, bo, co = nesterov(outer_wo, moment_wo, d_out)
     a2, b2, c2 = nesterov(outer_w2, moment_w2, d_down)
-    low_w = gather_rep(jnp.concatenate([ao, a2.reshape(rows, -1)], axis=1), n)
 
-    weights_wqkv = from_owners(dense_w[:, :, :w_qkv])
-    weights_w1 = from_owners(dense_w[:, :, w_qkv : w_qkv + w_ff])
-    weights_w3 = from_owners(dense_w[:, :, w_qkv + w_ff :])
-    weights_wo = from_owners(low_w[:, :, :w_o])
-    weights_w2 = from_owners(low_w[:, :, w_o:].reshape(n, -1, w_2))
+    q = rows_2 // rows
+    mine = jnp.concatenate(
+        [a0, a1, a3, ao] + [a2[k * rows : (k + 1) * rows] for k in range(q)], axis=1
+    )
+    got = gather_all(mine, "rep", n)
+    o1 = w_qkv
+    o3 = o1 + w_ff
+    oo = o3 + w_ff
+    o2 = oo + w_o
+    weights_wqkv = jnp.concatenate([got[j, :, :o1] for j in range(n)], axis=1)
+    weights_w1 = jnp.concatenate([got[j, :, o1:o3] for j in range(n)], axis=1)
+    weights_w3 = jnp.concatenate([got[j, :, o3:oo] for j in range(n)], axis=1)
+    weights_wo = jnp.concatenate([got[j, :, oo:o2] for j in range(n)], axis=1)
+    weights_w2 = jnp.concatenate(
+        [
+            jnp.concatenate(
+                [got[j, :, o2 + k * w_2 : o2 + (k + 1) * w_2] for k in range(q)], axis=0
+            )
+            for j in range(n)
+        ],
+        axis=1,
+    )
     return (
         weights_wqkv,
         weights_w1,

time: 457 us -> 297 us (0.65)
  waiting for transfers between devices: 325 us -> 162 us
  blocking collectives: 0 us -> 78.3 us
  local copies, waits for them, and re-layouts: 63.8 us -> 13.5 us
  between operations: 14.3 us -> 1.21 us
  starting transfers between devices: 22.4 us -> 13.4 us
    psum x1 -> x0, waiting for transfers between devices: 118 us -> none  [on_device(): coeff = lax.psum(own - total[rows:].reshape(rank, w_o + w_2) / n, 'shard')]
    all_to_all x0 -> x1, blocking collectives: none -> 78.3 us  [gather_all(): lax.all_to_all(jnp.broadcast_to(y[None], (n,) + y.shape), axis_name, 0, 0...]
    all_to_all x3 -> x2, waiting for transfers between devices: 207 us -> 162 us  [the longest x1 139 us: on_device(): lax.all_to_all(jnp.stack(send), 'rep', 0, 0, tiled=True)]
    concatenate x1 -> x4, local copies, waits for them, and re-layouts: 14.7 us -> 0.7 us  [the longest x1 0.63 us: on_device(): jnp.concatenate([a0, a1, a3, ao] + [a2[k * rows:(k + 1) * rows] for k in...]
    unnamed x39 -> x67, local copies, waits for them, and re-layouts: 22.1 us -> 8.17 us
    unnamed x0 -> x17, other arithmetic: none -> 13.4 us
    reshape x5 -> x0, local copies, waits for them, and re-layouts: 11.7 us -> none  [the longest x2 5.09 us: on_device(): send = jnp.concatenate([dense, coef_part.reshape(n, -1, width)], axis=1)]
    concatenate x4 -> x5, other arithmetic: 10.8 us -> 0.09 us  [the longest x4 0.07 us: on_device(): part = jnp.concatenate([po_b[j], p2_b[j]], axis=1)]
  transfers between devices with their start and end apart: 4 -> 2, of which waited for: 4 -> 2; matrix products, arithmetic and copies ran while one was open for 4% -> 2% of each run, Pallas kernels for 0% -> 0%
where the time goes in v2:
time: 297 us; the launch traced here: 295 us
  waiting for transfers between devices  162 us (55%)
  blocking collectives  78.3 us (26%)
  other arithmetic  19.5 us (7%)
  local copies, waits for them, and re-layouts  13.5 us (5%)
  starting transfers between devices  13.4 us (5%)
  matrix products  7.1 us (2%)
    all_to_all x1, waiting for transfers between devices, on_device(): lax.all_to_all(jnp.stack(send), 'rep', 0, 0, tiled=True)  139 us
    all_to_all x1, blocking collectives, gather_all(): lax.all_to_all(jnp.broadcast_to(y[None], (n,) + y.shape), axis_name, 0, 0...  78.3 us
    all_to_all x1, waiting for transfers between devices, gather_all(): lax.all_to_all(jnp.broadcast_to(y[None], (n,) + y.shape), axis_name, 0, 0...  22.4 us
    unnamed x17, other arithmetic  13.4 us
    all_to_all x1, starting transfers between devices, on_device(): lax.all_to_all(jnp.stack(send), 'rep', 0, 0, tiled=True)  8.22 us
    unnamed x67, local copies, waits for them, and re-layouts  8.17 us
  transfers between devices with their start and end apart: 2, of which 2 were waited for; matrix products, arithmetic and copies ran while one was open for 2% of the time, Pallas kernels for 0%

profile of v2, /device:TPU:6, one launch (start us, length us, event | category | flops | bytes accessed | tf_op | source)
XLA Modules:
  0.0 294.6 jit_solution(11743304589205869361)
XLA Ops:
  0.7 2.1 fusion.35
  2.9 2.0 fusion
  5.3 1.6 copy-done.4
  6.9 0.6 fusion.91
  7.6 1.1 fusion.33
  8.8 1.1 fusion.29
  9.9 1.2 fusion.25
  11.1 1.1 fusion.21
  12.2 1.2 fusion.17
  13.4 1.1 fusion.13
  14.5 1.2 fusion.9
  15.7 1.1 fusion.5
  16.8 8.2 %all-to-all-start = ((f32[8,144,2048]{2,1,0:T(8,128)}), f32[8,144,2048]{2,1,0:T(8,128)}, u32[]{:S(2)}, u32[]{:S(2)}) async-start(f32[8,144,2048]{2,1,0:T(8,128)} %fusion.5), calls=%async_computation | async-start | bytes 18874368 | tf_op jit(solution)/shard_map/all_to_all | solution.py:85
  25.6 139.2 %all-to-all-done = f32[8,144,2048]{2,1,0:T(8,128)} async-done(((f32[8,144,2048]{2,1,0:T(8,128)}), f32[8,144,2048]{2,1,0:T(8,128)}, u32[]{:S(2)}, u32[]{:S(2)}) %all-to-all-start) | async-done | bytes 9437216 | tf_op jit(solution)/shard_map/all_to_all | solution.py:85
  164.9 4.7 %reduce_sum.18 = f32[144,2048]{1,0:T(8,128)S(1)} reduce(f32[8,144,2048]{2,1,0:T(8,128)} %all-to-all-done, f32[]{:T(128)} %constant.4.clone.1), dimensions={0}, to_apply=%region_0.0 | reduce | flops 2064384 | bytes 10616836 | tf_op jit(solution)/shard_map/reduce_sum | solution.py:85
  169.6 1.7 broadcast_in_dim.4
  171.3 5.2 %all-to-all-start.1 = ((f32[16,64,512]{2,1,0:T(8,128)}), f32[16,64,512]{2,1,0:T(8,128)S(1)}, u32[]{:S(2)}, u32[]{:S(2)}) async-start(f32[16,64,512]{2,1,0:T(8,128)} %broadcast_in_dim.4), calls=%async_computation.1 | async-start | bytes 4194304 | tf_op jit(solution)/shard_map/all_to_all | solution.py:38
  176.5 2.0 convert_dynamic-update-slice_fusion.2
  178.6 2.1 convert_dynamic-update-slice_fusion.1
  180.7 1.0 convert_dynamic-update-slice_fusion
  181.7 22.4 %all-to-all-done.1 = f32[16,64,512]{2,1,0:T(8,128)S(1)} async-done(((f32[16,64,512]{2,1,0:T(8,128)}), f32[16,64,512]{2,1,0:T(8,128)S(1)}, u32[]{:S(2)}, u32[]{:S(2)}) %all-to-all-start.1) | async-done | bytes 2097184 | tf_op jit(solution)/shard_map/all_to_all | solution.py:38
  204.3 1.4 fusion.90
  205.8 1.0 constant_dynamic-update-slice_fusion.3
  206.8 0.6 constant_dynamic-update-slice_fusion.2
  207.5 0.6 constant_dynamic-update-slice_fusion.1
  208.1 0.6 constant_dynamic-update-slice_fusion
  208.7 1.9 broadcast_in_dim.5
  210.6 78.3 %all_to_all.15 = bf16[8,128,3072]{2,1,0:T(8,128)(2,1)S(1)} all-to-all(bf16[8,128,3072]{2,1,0:T(8,128)(2,1)S(1)} %broadcast_in_dim.5), channel_id=1, replica_groups=mesh['rep'=8,'shard'=16] {'rep'}, dimensions={0} | all-to-all | bytes 12582912 | tf_op jit(solution)/shard_map/all_to_all | solution.py:38
  289.6 0.9 copy-done.17
  290.7 0.8 copy-done.20
  291.7 1.1 copy-done.18
  293.4 1.2 copy-done.1
  (85 shorter events, 2.7 us)
Async XLA Ops:
  0.6 2.2 copy-start
  0.7 2.2 copy-start.8
  2.8 2.2 copy-start.6
  2.9 2.4 copy-start.5
  4.9 2.0 copy-start.4
  16.8 8.2 %copy-start.9 = (f32[128,256]{1,0:T(8,128)S(1)}, f32[128,256]{1,0:T(8,128)}, u32[]{:S(2)}) copy-start(f32[128,256]{1,0:T(8,128)} %param.25) | copy-start | bytes 393220
  16.8 8.2 %copy-start.14 = (f32[128,64]{0,1:T(8,128)S(1)}, f32[128,64]{0,1:T(8,128)}, u32[]{:S(2)}) copy-start(f32[128,64]{0,1:T(8,128)} %param.32) | copy-start | bytes 98308
  16.8 8.4 %copy-start.7 = (f32[384,256]{1,0:T(8,128)S(1)}, f32[384,256]{1,0:T(8,128)}, u32[]{:S(2)}) copy-start(f32[384,256]{1,0:T(8,128)} %param.26) | copy-start | bytes 1179652
  16.8 148.0 %all-to-all-start = ((f32[8,144,2048]{2,1,0:T(8,128)}), f32[8,144,2048]{2,1,0:T(8,128)}, u32[]{:S(2)}, u32[]{:S(2)}) async-start(f32[8,144,2048]{2,1,0:T(8,128)} %fusion.5), calls=%async_computation | async-start | bytes 18874368 | tf_op jit(solution)/shard_map/all_to_all | solution.py:85
  169.5 1.8 copy-start.2
  171.3 5.2 %copy-start.15 = (f32[128,512]{1,0:T(8,128)S(1)}, f32[128,512]{1,0:T(8,128)}, u32[]{:S(2)}) copy-start(f32[128,512]{1,0:T(8,128)} %param.22) | copy-start | bytes 786436
  171.3 7.2 %copy-start.10 = (f32[128,768]{1,0:T(8,128)S(1)}, f32[128,768]{1,0:T(8,128)}, u32[]{:S(2)}) copy-start(f32[128,768]{1,0:T(8,128)} %param.23) | copy-start | bytes 1179652
  171.3 32.9 %all-to-all-start.1 = ((f32[16,64,512]{2,1,0:T(8,128)}), f32[16,64,512]{2,1,0:T(8,128)S(1)}, u32[]{:S(2)}, u32[]{:S(2)}) async-start(f32[16,64,512]{2,1,0:T(8,128)} %broadcast_in_dim.4), calls=%async_computation.1 | async-start | bytes 4194304 | tf_op jit(solution)/shard_map/all_to_all | solution.py:38
  176.5 2.1 copy-start.3
  178.5 2.1 copy-start.11
  178.5 2.1 copy-start.12
  181.7 22.6 %copy-start.13 = (f32[384,256]{1,0:T(8,128)S(1)}, f32[384,256]{1,0:T(8,128)}, u32[]{:S(2)}) copy-start(f32[384,256]{1,0:T(8,128)} %param.31) | copy-start | bytes 1179652
  204.3 1.5 copy-start.16
  289.3 1.2 copy-start.17
  289.5 1.1 copy-start.21
  290.5 1.0 copy-start.20
  291.5 3.0 %copy-start.1 = (f32[1,384,2048]{2,1,0:T(8,128)S(1)}, f32[1,384,2048]{2,1,0:T(8,128)}, u32[]{:S(2)}) copy-start(f32[1,384,2048]{2,1,0:T(8,128)} %param.21) | copy-start | bytes 9437188
  291.7 1.1 copy-start.18
  291.7 1.7 copy-start.19

commit v3 on v2

--- a/solution.py
+++ b/solution.py
@@ -58,7 +58,6 @@
     basis_w2,
 ):
     n = lax.axis_size("rep")
-    n_shard = lax.axis_size("shard")
     w_qkv = outer_wqkv.shape[1]
     w_ff = outer_w1.shape[1]
     w_o = outer_wo.shape[1]
@@ -88,7 +87,7 @@
     folded = total[rows:]
     part = jnp.concatenate([folded[:, k * w_c : (k + 1) * w_c] for k in range(k_c)], axis=0)
     own = jnp.concatenate([project(basis_wo, outer_wo), project(basis_w2, outer_w2)], axis=1)
-    coeff = jnp.sum(gather_all(own - part / n, "shard", n_shard), axis=0)
+    coeff = jnp.sum(lax.all_gather(own - part / n, "shard", axis=0, tiled=False), axis=0)
 
     d_qkv = outer_wqkv - summed[:, :w_qkv] / n
     d_one = outer_w1 - summed[:, w_qkv : w_qkv + w_ff] / n
@@ -101,23 +100,21 @@
     ao, bo, co = nesterov(outer_wo, moment_wo, d_out)
     a2, b2, c2 = nesterov(outer_w2, moment_w2, d_down)
 
+    dense_w = gather_all(jnp.concatenate([a0, a1, a3], axis=1), "rep", n)
     q = rows_2 // rows
-    mine = jnp.concatenate(
-        [a0, a1, a3, ao] + [a2[k * rows : (k + 1) * rows] for k in range(q)], axis=1
+    low_w = gather_all(
+        jnp.concatenate([ao] + [a2[k * rows : (k + 1) * rows] for k in range(q)], axis=1), "rep", n
     )
-    got = gather_all(mine, "rep", n)
     o1 = w_qkv
     o3 = o1 + w_ff
-    oo = o3 + w_ff
-    o2 = oo + w_o
-    weights_wqkv = jnp.concatenate([got[j, :, :o1] for j in range(n)], axis=1)
-    weights_w1 = jnp.concatenate([got[j, :, o1:o3] for j in range(n)], axis=1)
-    weights_w3 = jnp.concatenate([got[j, :, o3:oo] for j in range(n)], axis=1)
-    weights_wo = jnp.concatenate([got[j, :, oo:o2] for j in range(n)], axis=1)
+    weights_wqkv = jnp.concatenate([dense_w[j, :, :o1] for j in range(n)], axis=1)
+    weights_w1 = jnp.concatenate([dense_w[j, :, o1:o3] for j in range(n)], axis=1)
+    weights_w3 = jnp.concatenate([dense_w[j, :, o3:] for j in range(n)], axis=1)
+    weights_wo = jnp.concatenate([low_w[j, :, :w_o] for j in range(n)], axis=1)
     weights_w2 = jnp.concatenate(
         [
             jnp.concatenate(
-                [got[j, :, o2 + k * w_2 : o2 + (k + 1) * w_2] for k in range(q)], axis=0
+                [low_w[j, :, w_o + k * w_2 : w_o + (k + 1) * w_2] for k in range(q)], axis=0
             )
             for j in range(n)
         ],

time: 297 us -> 273 us (0.919)
  waiting for transfers between devices: 162 us -> 66 us
  blocking collectives: 78.3 us -> 114 us
  local copies, waits for them, and re-layouts: 13.5 us -> 43.7 us
  between operations: 1.21 us -> 14.6 us
  other arithmetic: 19.5 us -> 11.5 us
    all_to_all x1 -> x0, waiting for transfers between devices: 139 us -> none  [on_device(): lax.all_to_all(jnp.stack(send), 'rep', 0, 0, tiled=True)]
    all_to_all x1 -> x2, waiting for transfers between devices: 22.4 us -> 66 us  [gather_all(): lax.all_to_all(jnp.broadcast_to(y[None], (n,) + y.shape), axis_name, 0, 0...]
    all_to_all x1, blocking collectives: 78.3 us -> 114 us  [on_device(): lax.all_to_all(jnp.stack(send), 'rep', 0, 0, tiled=True)]
    unnamed x67 -> x69, local copies, waits for them, and re-layouts: 8.17 us -> 34 us
    unnamed x17 -> x14, other arithmetic: 13.4 us -> 0.91 us
    all_to_all x1 -> x2, starting transfers between devices: 5.17 us -> 16.3 us  [gather_all(): lax.all_to_all(jnp.broadcast_to(y[None], (n,) + y.shape), axis_name, 0, 0...]
    all_to_all x1 -> x0, starting transfers between devices: 8.22 us -> none  [on_device(): lax.all_to_all(jnp.stack(send), 'rep', 0, 0, tiled=True)]
    concatenate x4 -> x5, local copies, waits for them, and re-layouts: 0.7 us -> 4.36 us  [the longest x1 1.79 us: on_device(): weights_w3 = jnp.concatenate([dense_w[j, :, o3:] for j in range(n)], axis=1)]
  transfers between devices with their start and end apart: 2 -> 3, of which waited for: 2 -> 2; matrix products, arithmetic and copies ran while one was open for 2% -> 10% of each run, Pallas kernels for 0% -> 0%
where the time goes in v3:
time: 273 us; the launch traced here: 272 us
  blocking collectives  114 us (42%)
  waiting for transfers between devices  66 us (24%)
  local copies, waits for them, and re-layouts  43.7 us (16%)
  starting transfers between devices  16.3 us (6%)
  between operations  14.6 us (5%)
  other arithmetic  11.5 us (4%)
  matrix products  5.6 us (2%)
    all_to_all x1, blocking collectives, on_device(): lax.all_to_all(jnp.stack(send), 'rep', 0, 0, tiled=True)  114 us
    all_to_all x2, waiting for transfers between devices, gather_all(): lax.all_to_all(jnp.broadcast_to(y[None], (n,) + y.shape), axis_name, 0, 0...  66 us
    unnamed x69, local copies, waits for them, and re-layouts  34 us
    all_to_all x2, starting transfers between devices, gather_all(): lax.all_to_all(jnp.broadcast_to(y[None], (n,) + y.shape), axis_name, 0, 0...  16.3 us
  transfers between devices with their start and end apart: 3, of which 2 were waited for; matrix products, arithmetic and copies ran while one was open for 10% of the time, Pallas kernels for 0%

profile of v3, /device:TPU:6, one launch (start us, length us, event | category | flops | bytes accessed | tf_op | source)
XLA Modules:
  0.0 272.0 jit_solution(12430895486720418277)
XLA Ops:
  7.2 2.1 fusion.35
  9.4 2.0 fusion
  11.8 1.6 copy-done.3
  15.2 114.4 %all_to_all.15 = f32[8,144,2048]{2,1,0:T(8,128)} all-to-all(f32[8,144,2048]{2,1,0:T(8,128)S(1)} %fusion.5), channel_id=1, replica_groups=mesh['rep'=8,'shard'=16] {'rep'}, dimensions={0} | all-to-all | bytes 18874368 | tf_op jit(solution)/shard_map/all_to_all | solution.py:84
  129.6 4.7 %reduce_sum.18 = f32[144,2048]{1,0:T(8,128)S(1)} reduce(f32[8,144,2048]{2,1,0:T(8,128)} %all_to_all.15, f32[]{:T(128)} %constant.4.clone.1), dimensions={0}, to_apply=%region_0.0 | reduce | flops 2064384 | bytes 10616836 | tf_op jit(solution)/shard_map/reduce_sum | solution.py:84
  135.8 2.2 fusion.93
  138.1 2.6 broadcast_in_dim.4
  140.7 6.3 %all-to-all-start.1 = ((bf16[8,128,2048]{2,1,0:T(8,128)(2,1)}), bf16[8,128,2048]{2,1,0:T(8,128)(2,1)}, u32[]{:S(2)}, u32[]{:S(2)}) async-start(bf16[8,128,2048]{2,1,0:T(8,128)(2,1)} %broadcast_in_dim.4), calls=%async_computation.1 | async-start | bytes 8388608 | tf_op jit(solution)/shard_map/all_to_all | solution.py:38
  148.9 53.9 %all-to-all-done.1 = bf16[8,128,2048]{2,1,0:T(8,128)(2,1)} async-done(((bf16[8,128,2048]{2,1,0:T(8,128)(2,1)}), bf16[8,128,2048]{2,1,0:T(8,128)(2,1)}, u32[]{:S(2)}, u32[]{:S(2)}) %all-to-all-start.1) | async-done | bytes 4194336 | tf_op jit(solution)/shard_map/all_to_all | solution.py:38
  202.8 0.9 fusion.63
  203.7 0.9 fusion.62
  204.6 0.9 fusion.61
  205.5 0.9 fusion.60
  206.5 0.9 fusion.59
  207.4 0.9 fusion.58
  208.3 0.9 fusion.57
  209.2 2.2 fusion.47
  211.4 1.8 reduce_sum.19
  214.4 1.6 broadcast_in_dim.5
  216.0 9.9 %all-to-all-start.2 = ((bf16[8,128,1024]{2,1,0:T(8,128)(2,1)}), bf16[8,128,1024]{2,1,0:T(8,128)(2,1)S(1)}, u32[]{:S(2)}, u32[]{:S(2)}) async-start(bf16[8,128,1024]{2,1,0:T(8,128)(2,1)} %broadcast_in_dim.5), calls=%async_computation.2 | async-start | bytes 4194304 | tf_op jit(solution)/shard_map/all_to_all | solution.py:38
  226.0 1.6 fusion.56
  227.5 1.8 fusion.46
  229.3 1.8 fusion.45
  231.1 1.8 fusion.44
  232.9 1.8 fusion.43
  234.7 1.8 fusion.42
  236.5 1.8 fusion.41
  238.3 1.8 fusion.40
  243.4 12.1 %all-to-all-done.2 = bf16[8,128,1024]{2,1,0:T(8,128)(2,1)S(1)} async-done(((bf16[8,128,1024]{2,1,0:T(8,128)(2,1)}), bf16[8,128,1024]{2,1,0:T(8,128)(2,1)S(1)}, u32[]{:S(2)}, u32[]{:S(2)}) %all-to-all-start.2) | async-done | bytes 2097184 | tf_op jit(solution)/shard_map/all_to_all | solution.py:38
  255.7 1.2 copy-done.2
  257.0 1.1 constant_dynamic-update-slice_fusion.7
  258.2 1.1 constant_dynamic-update-slice_fusion.6
  (92 shorter events, 16.1 us)
Async XLA Ops:
  7.2 2.2 copy-start
  7.2 2.2 copy-start.7
  9.3 2.2 copy-start.5
  9.4 2.4 copy-start.4
  11.5 2.0 copy-start.3
  129.6 4.7 %copy-start.14 = (f32[128,512]{1,0:T(8,128)S(1)}, f32[128,512]{1,0:T(8,128)}, u32[]{:S(2)}) copy-start(f32[128,512]{1,0:T(8,128)} %param.22) | copy-start | bytes 786436
  129.6 4.7 %copy-start.15 = (f32[128,512]{1,0:T(8,128)S(1)}, f32[128,512]{1,0:T(8,128)}, u32[]{:S(2)}) copy-start(f32[128,512]{1,0:T(8,128)} %param.27) | copy-start | bytes 786436
  134.4 1.0 copy-start.9
  134.4 1.3 copy-start.10
  134.4 1.4 copy-start.11
  140.7 6.3 %copy-start.8 = (f32[128,256]{1,0:T(8,128)S(1)}, f32[128,256]{1,0:T(8,128)}, u32[]{:S(2)}) copy-start(f32[128,256]{1,0:T(8,128)} %param.25) | copy-start | bytes 393220
  140.7 6.3 %copy-start.13 = (f32[128,64]{0,1:T(8,128)S(1)}, f32[128,64]{0,1:T(8,128)}, u32[]{:S(2)}) copy-start(f32[128,64]{0,1:T(8,128)} %param.32) | copy-start | bytes 98308
  140.7 6.6 %copy-start.6 = (f32[384,256]{1,0:T(8,128)S(1)}, f32[384,256]{1,0:T(8,128)}, u32[]{:S(2)}) copy-start(f32[384,256]{1,0:T(8,128)} %param.26) | copy-start | bytes 1179652
  140.7 62.1 %all-to-all-start.1 = ((bf16[8,128,2048]{2,1,0:T(8,128)(2,1)}), bf16[8,128,2048]{2,1,0:T(8,128)(2,1)}, u32[]{:S(2)}, u32[]{:S(2)}) async-start(bf16[8,128,2048]{2,1,0:T(8,128)(2,1)} %broadcast_in_dim.4), calls=%async_computation.1 | async-start | bytes 8388608 | tf_op jit(solution)/shard_map/all_to_all | solution.py:38
  147.0 64.4 %all-gather.2.cloned.1.call-start = ((), (), s32[]{:S(2)}) async-start(), calls=%async_computation.3 | async-start | bytes 2228224 | tf_op jit(solution)/shard_map/all_gather | solution.py:90
  147.2 1.4 copy-start.12
  147.6 1.2 copy-start.16
  209.2 2.2 copy-start.18
  216.0 39.4 %all-to-all-start.2 = ((bf16[8,128,1024]{2,1,0:T(8,128)(2,1)}), bf16[8,128,1024]{2,1,0:T(8,128)(2,1)S(1)}, u32[]{:S(2)}, u32[]{:S(2)}) async-start(bf16[8,128,1024]{2,1,0:T(8,128)(2,1)} %broadcast_in_dim.5), calls=%async_computation.2 | async-start | bytes 4194304 | tf_op jit(solution)/shard_map/all_to_all | solution.py:38
  255.5 1.4 copy-start.2
  256.9 8.3 %copy-start.1 = (f32[1,384,2048]{2,1,0:T(8,128)S(1)}, f32[1,384,2048]{2,1,0:T(8,128)}, u32[]{:S(2)}) copy-start(f32[1,384,2048]{2,1,0:T(8,128)} %param.21) | copy-start | bytes 9437188
  257.0 7.4 %copy-start.17 = (bf16[384,2048]{1,0:T(8,128)(2,1)}, bf16[384,2048]{1,0:T(8,128)(2,1)S(1)}, u32[]{:S(2)}) copy-start(bf16[384,2048]{1,0:T(8,128)(2,1)S(1)} %maximum_dynamic-update-slice_fusion) | copy-start | bytes 4718596
  264.4 0.8 copy-start.19
Sparse Core Ops, SparseCore 0:
  150.1 58.7 all-gather.1

commit v4 on v3

--- a/solution.py
+++ b/solution.py
@@ -64,13 +64,15 @@
     w_2 = outer_w2.shape[1]
     rows = inner_wqkv.shape[1]
     rows_2 = outer_w2.shape[0]
-    rank = basis_wo.shape[1]
-    width = w_qkv + 2 * w_ff
+
+    s_qkv = lax.psum_scatter(
+        jnp.stack(owner_blocks(inner_wqkv[0], n)), "rep", scatter_dimension=0, tiled=True
+    )[0]
+    width = 2 * w_ff
     w_c = w_o + w_2
     k_c = width // w_c
-    r_c = rank // k_c
-
-    qkv_b = owner_blocks(inner_wqkv[0], n)
+    rank = basis_wo.shape[1]
+    r_c = -(-rank // (8 * k_c)) * 8
     one_b = owner_blocks(inner_w1[0], n)
     three_b = owner_blocks(inner_w3[0], n)
     po_b = owner_blocks(project(basis_wo, inner_wo[0]), n)
@@ -78,20 +80,21 @@
     send = []
     for j in range(n):
         part = jnp.concatenate([po_b[j], p2_b[j]], axis=1)
+        part = jnp.pad(part, ((0, k_c * r_c - rank), (0, 0)))
         folded = jnp.concatenate([part[k * r_c : (k + 1) * r_c] for k in range(k_c)], axis=1)
-        dense = jnp.concatenate([qkv_b[j], one_b[j], three_b[j]], axis=1)
+        dense = jnp.concatenate([one_b[j], three_b[j]], axis=1)
         send.append(jnp.concatenate([dense, folded], axis=0))
     total = jnp.sum(lax.all_to_all(jnp.stack(send), "rep", 0, 0, tiled=True), axis=0)
 
     summed = total[:rows]
     folded = total[rows:]
-    part = jnp.concatenate([folded[:, k * w_c : (k + 1) * w_c] for k in range(k_c)], axis=0)
+    part = jnp.concatenate([folded[:, k * w_c : (k + 1) * w_c] for k in range(k_c)], axis=0)[:rank]
     own = jnp.concatenate([project(basis_wo, outer_wo), project(basis_w2, outer_w2)], axis=1)
     coeff = jnp.sum(lax.all_gather(own - part / n, "shard", axis=0, tiled=False), axis=0)
 
-    d_qkv = outer_wqkv - summed[:, :w_qkv] / n
-    d_one = outer_w1 - summed[:, w_qkv : w_qkv + w_ff] / n
-    d_three = outer_w3 - summed[:, w_qkv + w_ff :] / n
+    d_qkv = outer_wqkv - s_qkv / n
+    d_one = outer_w1 - summed[:, :w_ff] / n
+    d_three = outer_w3 - summed[:, w_ff:] / n
     a0, b0, c0 = nesterov(outer_wqkv, moment_wqkv, d_qkv)
     a1, b1, c1 = nesterov(outer_w1, moment_w1, d_one)
     a3, b3, c3 = nesterov(outer_w3, moment_w3, d_three)

time: 273 us -> 336 us (1.23)
  waiting for transfers between devices: 66 us -> 220 us
  blocking collectives: 114 us -> 0 us
  other arithmetic: 11.5 us -> 19.3 us
  starting transfers between devices: 16.3 us -> 23.3 us
  local copies, waits for them, and re-layouts: 43.7 us -> 50.3 us
    reduce_scatter x0 -> x1, waiting for transfers between devices: none -> 154 us  [on_device(): lax.psum_scatter(jnp.stack(owner_blocks(inner_wqkv[0], n)), 'rep', scatte...]
    all_to_all x1 -> x0, blocking collectives: 114 us -> none  [on_device(): lax.all_to_all(jnp.stack(send), 'rep', 0, 0, tiled=True)]
    all_to_all x0 -> x1, starting transfers between devices: none -> 8.09 us  [on_device(): lax.all_to_all(jnp.stack(send), 'rep', 0, 0, tiled=True)]
    unnamed x14, other arithmetic: 0.91 us -> 7.53 us
    unnamed x69 -> x78, local copies, waits for them, and re-layouts: 34 us -> 39.3 us
  transfers between devices with their start and end apart: 3 -> 5, of which waited for: 2 -> 3; matrix products, arithmetic and copies ran while one was open for 10% -> 10% of each run, Pallas kernels for 0% -> 0%
where the time goes in v4:
time: 336 us; the launch traced here: 335 us
  waiting for transfers between devices  220 us (65%)
  local copies, waits for them, and re-layouts  50.3 us (15%)
  starting transfers between devices  23.3 us (7%)
  other arithmetic  19.3 us (6%)
  between operations  16.1 us (5%)
  matrix products  5.6 us (2%)
    reduce_scatter x1, waiting for transfers between devices, on_device(): lax.psum_scatter(jnp.stack(owner_blocks(inner_wqkv[0], n)), 'rep', scatte...  154 us
    all_to_all x2, waiting for transfers between devices, gather_all(): lax.all_to_all(jnp.broadcast_to(y[None], (n,) + y.shape), axis_name, 0, 0...  66.3 us
    unnamed x78, local copies, waits for them, and re-layouts  39.3 us
    all_to_all x2, starting transfers between devices, gather_all(): lax.all_to_all(jnp.broadcast_to(y[None], (n,) + y.shape), axis_name, 0, 0...  15.2 us
    all_to_all x1, starting transfers between devices, on_device(): lax.all_to_all(jnp.stack(send), 'rep', 0, 0, tiled=True)  8.09 us
    unnamed x14, other arithmetic  7.53 us
  transfers between devices with their start and end apart: 5, of which 3 were waited for; matrix products, arithmetic and copies ran while one was open for 10% of the time, Pallas kernels for 0%

profile of v4, /device:TPU:6, one launch (start us, length us, event | category | flops | bytes accessed | tf_op | source)
XLA Modules:
  0.0 335.0 jit_solution(5166479771648061769)
XLA Ops:
  8.0 2.1 fusion.2
  10.2 2.0 fusion
  12.6 1.5 copy-done.4
  15.8 1.1 fusion.4
  18.0 1.1 fusion.6
  21.1 1.1 fusion.9
  23.2 1.1 fusion.11
  24.3 8.1 %all-to-all-start = ((f32[8,152,1536]{2,1,0:T(8,128)}), f32[8,152,1536]{2,1,0:T(8,128)}, u32[]{:S(2)}, u32[]{:S(2)}) async-start(f32[8,152,1536]{2,1,0:T(8,128)} %fusion.11), calls=%async_computation.1 | async-start | bytes 14942208 | tf_op jit(solution)/shard_map/all_to_all | solution.py:87
  32.4 1.1 fusion.21
  36.6 1.3 copy-done.5
  37.9 154.1 %reduce-scatter.2.cloned.1.call-done = f32[1,128,512]{2,1,0:T(8,128)} async-done(((f32[8,128,512]{2,1,0:T(8,128)}), f32[1,128,512]{2,1,0:T(8,128)}) %reduce-scatter.2.cloned.1.call-update) | async-done | bytes 262160 | tf_op jit(solution)/shard_map/reduce_scatter | solution.py:68
  192.0 1.8 fusion.68
  193.8 4.0 %reduce_sum.18 = f32[152,1536]{1,0:T(8,128)S(1)} reduce(f32[8,152,1536]{2,1,0:T(8,128)} %all-to-all-done, f32[]{:T(128)} %constant.8.clone.1), dimensions={0}, to_apply=%region_1.2 | reduce | flops 1634304 | bytes 8404996 | tf_op jit(solution)/shard_map/reduce_sum | solution.py:87
  197.9 2.3 fusion.69
  200.2 2.6 broadcast_in_dim.4
  202.7 5.6 %all-to-all-start.1 = ((bf16[8,128,2048]{2,1,0:T(8,128)(2,1)}), bf16[8,128,2048]{2,1,0:T(8,128)(2,1)}, u32[]{:S(2)}, u32[]{:S(2)}) async-start(bf16[8,128,2048]{2,1,0:T(8,128)(2,1)} %broadcast_in_dim.4), calls=%async_computation.2 | async-start | bytes 8388608 | tf_op jit(solution)/shard_map/all_to_all | solution.py:38
  210.2 54.2 %all-to-all-done.1 = bf16[8,128,2048]{2,1,0:T(8,128)(2,1)} async-done(((bf16[8,128,2048]{2,1,0:T(8,128)(2,1)}), bf16[8,128,2048]{2,1,0:T(8,128)(2,1)}, u32[]{:S(2)}, u32[]{:S(2)}) %all-to-all-start.1) | async-done | bytes 4194336 | tf_op jit(solution)/shard_map/all_to_all | solution.py:38
  270.9 2.2 fusion.29
  273.1 1.8 reduce_sum.19
  276.0 1.6 broadcast_in_dim.5
  277.7 9.6 %all-to-all-start.2 = ((bf16[8,128,1024]{2,1,0:T(8,128)(2,1)}), bf16[8,128,1024]{2,1,0:T(8,128)(2,1)S(1)}, u32[]{:S(2)}, u32[]{:S(2)}) async-start(bf16[8,128,1024]{2,1,0:T(8,128)(2,1)} %broadcast_in_dim.5), calls=%async_computation.3 | async-start | bytes 4194304 | tf_op jit(solution)/shard_map/all_to_all | solution.py:38
  287.3 1.6 fusion.40
  288.8 1.8 fusion.28
  290.6 1.8 fusion.27
  292.4 1.8 fusion.26
  294.2 1.8 fusion.25
  296.0 1.8 fusion.24
  297.8 1.8 fusion.23
  299.6 1.8 fusion.22
  304.7 12.1 %all-to-all-done.2 = bf16[8,128,1024]{2,1,0:T(8,128)(2,1)S(1)} async-done(((bf16[8,128,1024]{2,1,0:T(8,128)(2,1)}), bf16[8,128,1024]{2,1,0:T(8,128)(2,1)S(1)}, u32[]{:S(2)}, u32[]{:S(2)}) %all-to-all-start.2) | async-done | bytes 2097184 | tf_op jit(solution)/shard_map/all_to_all | solution.py:38
  316.8 1.3 copy-done.2
  318.2 1.5 slice_bitcast_fusion.34
  (117 shorter events, 29.8 us)
Async XLA Ops:
  8.0 2.2 copy-start
  8.0 2.2 copy-start.8
  12.2 1.9 copy-start.4
  12.4 2.7 copy-start.3
  24.3 169.5 %all-to-all-start = ((f32[8,152,1536]{2,1,0:T(8,128)}), f32[8,152,1536]{2,1,0:T(8,128)}, u32[]{:S(2)}, u32[]{:S(2)}) async-start(f32[8,152,1536]{2,1,0:T(8,128)} %fusion.11), calls=%async_computation.1 | async-start | bytes 14942208 | tf_op jit(solution)/shard_map/all_to_all | solution.py:87
  32.4 159.6 %reduce-scatter.2.cloned.1.call-start = ((), (), s32[]{:S(2)}) async-start(), calls=%async_computation.4 | async-start | bytes 2359296 | tf_op jit(solution)/shard_map/reduce_scatter | solution.py:68
  32.4 4.0 %copy-start.6 = (f32[1,128,4096]{2,1,0:T(8,128)S(1)}, f32[1,128,4096]{2,1,0:T(8,128)}, u32[]{:S(2)}) copy-start(f32[1,128,4096]{2,1,0:T(8,128)} %param.17) | copy-start | bytes 6291460
  36.4 155.5 %copy-start.15 = (f32[128,512]{1,0:T(8,128)S(1)}, f32[128,512]{1,0:T(8,128)}, u32[]{:S(2)}) copy-start(f32[128,512]{1,0:T(8,128)} %param.22) | copy-start | bytes 786436
  36.5 155.5 %copy-start.16 = (f32[128,512]{1,0:T(8,128)S(1)}, f32[128,512]{1,0:T(8,128)}, u32[]{:S(2)}) copy-start(f32[128,512]{1,0:T(8,128)} %param.27) | copy-start | bytes 786436
  36.6 1.3 copy-start.5
  193.8 4.0 %copy-start.10 = (f32[128,768]{1,0:T(8,128)S(1)}, f32[128,768]{1,0:T(8,128)}, u32[]{:S(2)}) copy-start(f32[128,768]{1,0:T(8,128)} %param.23) | copy-start | bytes 1179652
  193.8 4.0 %copy-start.11 = (f32[128,768]{1,0:T(8,128)S(1)}, f32[128,768]{1,0:T(8,128)}, u32[]{:S(2)}) copy-start(f32[128,768]{1,0:T(8,128)} %param.28) | copy-start | bytes 1179652
  193.8 4.0 %copy-start.12 = (f32[128,768]{1,0:T(8,128)S(1)}, f32[128,768]{1,0:T(8,128)}, u32[]{:S(2)}) copy-start(f32[128,768]{1,0:T(8,128)} %param.24) | copy-start | bytes 1179652
  202.7 5.6 %copy-start.9 = (f32[128,256]{1,0:T(8,128)S(1)}, f32[128,256]{1,0:T(8,128)}, u32[]{:S(2)}) copy-start(f32[128,256]{1,0:T(8,128)} %param.25) | copy-start | bytes 393220
  202.7 5.6 %copy-start.14 = (f32[128,64]{0,1:T(8,128)S(1)}, f32[128,64]{0,1:T(8,128)}, u32[]{:S(2)}) copy-start(f32[128,64]{0,1:T(8,128)} %param.32) | copy-start | bytes 98308
  202.7 5.9 %copy-start.7 = (f32[384,256]{1,0:T(8,128)S(1)}, f32[384,256]{1,0:T(8,128)}, u32[]{:S(2)}) copy-start(f32[384,256]{1,0:T(8,128)} %param.26) | copy-start | bytes 1179652
  202.7 61.7 %all-to-all-start.1 = ((bf16[8,128,2048]{2,1,0:T(8,128)(2,1)}), bf16[8,128,2048]{2,1,0:T(8,128)(2,1)}, u32[]{:S(2)}, u32[]{:S(2)}) async-start(bf16[8,128,2048]{2,1,0:T(8,128)(2,1)} %broadcast_in_dim.4), calls=%async_computation.2 | async-start | bytes 8388608 | tf_op jit(solution)/shard_map/all_to_all | solution.py:38
  208.3 1.6 copy-start.13
  208.3 1.8 copy-start.17
  208.3 64.7 %all-gather.3.cloned.1.call-start = ((), (), s32[]{:S(2)}) async-start(), calls=%async_computation.5 | async-start | bytes 2228224 | tf_op jit(solution)/shard_map/all_gather | solution.py:93
  270.9 2.2 copy-start.19
  277.7 39.1 %all-to-all-start.2 = ((bf16[8,128,1024]{2,1,0:T(8,128)(2,1)}), bf16[8,128,1024]{2,1,0:T(8,128)(2,1)S(1)}, u32[]{:S(2)}, u32[]{:S(2)}) async-start(bf16[8,128,1024]{2,1,0:T(8,128)(2,1)} %broadcast_in_dim.5), calls=%async_computation.3 | async-start | bytes 4194304 | tf_op jit(solution)/shard_map/all_to_all | solution.py:38
  316.8 1.3 copy-start.2
  318.2 9.4 %copy-start.1 = (f32[1,384,2048]{2,1,0:T(8,128)S(1)}, f32[1,384,2048]{2,1,0:T(8,128)}, u32[]{:S(2)}) copy-start(f32[1,384,2048]{2,1,0:T(8,128)} %param.21) | copy-start | bytes 9437188
  319.9 6.8 %copy-start.18 = (bf16[384,2048]{1,0:T(8,128)(2,1)}, bf16[384,2048]{1,0:T(8,128)(2,1)S(1)}, u32[]{:S(2)}) copy-start(bf16[384,2048]{1,0:T(8,128)(2,1)S(1)} %maximum_dynamic-update-slice_fusion) | copy-start | bytes 4718596
  326.8 0.8 copy-start.20
Sparse Core Ops, SparseCore 0:
  38.0 153.9 reduce-scatter.1
Sparse Core Ops, SparseCore 1:
  211.1 58.9 all-gather.2

commit v5 on v3

--- a/solution.py
+++ b/solution.py
@@ -64,30 +64,19 @@
     w_2 = outer_w2.shape[1]
     rows = inner_wqkv.shape[1]
     rows_2 = outer_w2.shape[0]
-    rank = basis_wo.shape[1]
-    width = w_qkv + 2 * w_ff
-    w_c = w_o + w_2
-    k_c = width // w_c
-    r_c = rank // k_c
+
+    po_b = owner_blocks(project(basis_wo, inner_wo[0]), n)
+    p2_b = owner_blocks(project(basis_w2, inner_w2[0]), n)
+    coef_send = jnp.stack([jnp.concatenate([po_b[j], p2_b[j]], axis=1) for j in range(n)])
+    part = jnp.sum(lax.all_to_all(coef_send, "rep", 0, 0, tiled=True), axis=0)
+    own = jnp.concatenate([project(basis_wo, outer_wo), project(basis_w2, outer_w2)], axis=1)
+    coeff = jnp.sum(lax.all_gather(own - part / n, "shard", axis=0, tiled=False), axis=0)
 
     qkv_b = owner_blocks(inner_wqkv[0], n)
     one_b = owner_blocks(inner_w1[0], n)
     three_b = owner_blocks(inner_w3[0], n)
-    po_b = owner_blocks(project(basis_wo, inner_wo[0]), n)
-    p2_b = owner_blocks(project(basis_w2, inner_w2[0]), n)
-    send = []
-    for j in range(n):
-        part = jnp.concatenate([po_b[j], p2_b[j]], axis=1)
-        folded = jnp.concatenate([part[k * r_c : (k + 1) * r_c] for k in range(k_c)], axis=1)
-        dense = jnp.concatenate([qkv_b[j], one_b[j], three_b[j]], axis=1)
-        send.append(jnp.concatenate([dense, folded], axis=0))
-    total = jnp.sum(lax.all_to_all(jnp.stack(send), "rep", 0, 0, tiled=True), axis=0)
-
-    summed = total[:rows]
-    folded = total[rows:]
-    part = jnp.concatenate([folded[:, k * w_c : (k + 1) * w_c] for k in range(k_c)], axis=0)
-    own = jnp.concatenate([project(basis_wo, outer_wo), project(basis_w2, outer_w2)], axis=1)
-    coeff = jnp.sum(lax.all_gather(own - part / n, "shard", axis=0, tiled=False), axis=0)
+    send = jnp.stack([jnp.concatenate([qkv_b[j], one_b[j], three_b[j]], axis=1) for j in range(n)])
+    summed = jnp.sum(lax.all_to_all(send, "rep", 0, 0, tiled=True), axis=0)
 
     d_qkv = outer_wqkv - summed[:, :w_qkv] / n
     d_one = outer_w1 - summed[:, w_qkv : w_qkv + w_ff] / n

time: 273 us -> 302 us (1.11)
  waiting for transfers between devices: 66 us -> 192 us
  blocking collectives: 114 us -> 0 us
  other arithmetic: 11.5 us -> 25.2 us
  starting transfers between devices: 16.3 us -> 29.8 us
  local copies, waits for them, and re-layouts: 43.7 us -> 32.3 us
    all_to_all x1 -> x0, blocking collectives: 114 us -> none  [on_device(): lax.all_to_all(jnp.stack(send), 'rep', 0, 0, tiled=True)]
    all_to_all x0 -> x2, waiting for transfers between devices: none -> 72.5 us  [the longest x1 71.1 us: on_device(): summed = jnp.sum(lax.all_to_all(send, 'rep', 0, 0, tiled=True), axis=0)]
    all_gather x1, waiting for transfers between devices: 0.01 us -> 47 us  [on_device(): lax.all_gather(own - part / n, 'shard', axis=0, tiled=False)]
    all_to_all x0 -> x2, starting transfers between devices: none -> 15.6 us  [the longest x1 8.09 us: on_device(): part = jnp.sum(lax.all_to_all(coef_send, 'rep', 0, 0, tiled=True), axis=0)]
    unnamed x14 -> x21, other arithmetic: 0.91 us -> 12.4 us
    unnamed x69 -> x73, local copies, waits for them, and re-layouts: 34 us -> 23 us
    all_to_all x2, waiting for transfers between devices: 66 us -> 72.7 us  [gather_all(): lax.all_to_all(jnp.broadcast_to(y[None], (n,) + y.shape), axis_name, 0, 0...]
  transfers between devices with their start and end apart: 3 -> 5, of which waited for: 2 -> 5; matrix products, arithmetic and copies ran while one was open for 10% -> 10% of each run, Pallas kernels for 0% -> 0%
where the time goes in v5:
time: 302 us; the launch traced here: 301 us
  waiting for transfers between devices  192 us (64%)
  local copies, waits for them, and re-layouts  32.3 us (11%)
  starting transfers between devices  29.8 us (10%)
  other arithmetic  25.2 us (8%)
  between operations  14.6 us (5%)
  matrix products  7.04 us (2%)
    all_to_all x2, waiting for transfers between devices, gather_all(): lax.all_to_all(jnp.broadcast_to(y[None], (n,) + y.shape), axis_name, 0, 0...  72.7 us
    all_to_all x1, waiting for transfers between devices, on_device(): summed = jnp.sum(lax.all_to_all(send, 'rep', 0, 0, tiled=True), axis=0)  71.1 us
    all_gather x1, waiting for transfers between devices, on_device(): lax.all_gather(own - part / n, 'shard', axis=0, tiled=False)  47 us
    unnamed x73, local copies, waits for them, and re-layouts  23 us
    all_to_all x2, starting transfers between devices, gather_all(): lax.all_to_all(jnp.broadcast_to(y[None], (n,) + y.shape), axis_name, 0, 0...  14.2 us
    unnamed x21, other arithmetic  12.4 us
    all_to_all x1, starting transfers between devices, on_device(): part = jnp.sum(lax.all_to_all(coef_send, 'rep', 0, 0, tiled=True), axis=0)  8.09 us
    all_to_all x1, starting transfers between devices, on_device(): summed = jnp.sum(lax.all_to_all(send, 'rep', 0, 0, tiled=True), axis=0)  7.53 us
  transfers between devices with their start and end apart: 5, of which 5 were waited for; matrix products, arithmetic and copies ran while one was open for 10% of the time, Pallas kernels for 0%

profile of v5, /device:TPU:6, one launch (start us, length us, event | category | flops | bytes accessed | tf_op | source)
XLA Modules:
  0.0 301.1 jit_solution(101036166148740145)
XLA Ops:
  7.2 2.1 fusion.10
  9.4 2.0 fusion
  16.8 8.1 %all-to-all-start.2 = ((f32[8,64,512]{2,1,0:T(8,128)}), f32[8,64,512]{2,1,0:T(8,128)S(1)}, u32[]{:S(2)}, u32[]{:S(2)}) async-start(f32[8,64,512]{2,1,0:T(8,128)} %fusion.46), calls=%async_computation.2 | async-start | bytes 2097152 | tf_op jit(solution)/shard_map/all_to_all | solution.py:71
  25.1 1.7 copy-done.2
  26.8 2.5 fusion.54
  29.4 1.1 fusion.2
  30.5 1.1 fusion.3
  32.6 1.1 fusion.5
  33.7 1.1 fusion.6
  34.8 1.1 fusion.7
  35.9 1.1 fusion.8
  37.0 1.1 fusion.9
  38.1 1.4 all-to-all-done.2
  39.5 7.5 %all-to-all-start = ((f32[8,128,2048]{2,1,0:T(8,128)}), f32[8,128,2048]{2,1,0:T(8,128)}, u32[]{:S(2)}, u32[]{:S(2)}) async-start(f32[8,128,2048]{2,1,0:T(8,128)} %fusion.9), calls=%async_computation | async-start | bytes 16777216 | tf_op jit(solution)/shard_map/all_to_all | solution.py:79
  48.9 47.0 %all-gather.2.cloned.1.call-done = f32[16,64,512]{2,1,0:T(8,128)} async-done(((f32[1,64,512]{2,1,0:T(8,128)}), f32[16,64,512]{2,1,0:T(8,128)}) %all-gather.2.cloned.1.call-update) | async-done | bytes 2097168 | tf_op jit(solution)/shard_map/all_gather | solution.py:73
  96.0 1.8 reduce_sum.29
  97.8 1.3 fusion.50
  99.1 1.1 fusion.49
  100.4 71.1 %all-to-all-done = f32[8,128,2048]{2,1,0:T(8,128)} async-done(((f32[8,128,2048]{2,1,0:T(8,128)}), f32[8,128,2048]{2,1,0:T(8,128)}, u32[]{:S(2)}, u32[]{:S(2)}) %all-to-all-start) | async-done | bytes 8388640 | tf_op jit(solution)/shard_map/all_to_all | solution.py:79
  171.5 1.6 broadcast_in_dim.5
  173.1 6.9 %all-to-all-start.3 = ((bf16[8,128,1024]{2,1,0:T(8,128)(2,1)}), bf16[8,128,1024]{2,1,0:T(8,128)(2,1)S(1)}, u32[]{:S(2)}, u32[]{:S(2)}) async-start(bf16[8,128,1024]{2,1,0:T(8,128)(2,1)} %broadcast_in_dim.5), calls=%async_computation.3 | async-start | bytes 4194304 | tf_op jit(solution)/shard_map/all_to_all | solution.py:38
  180.0 4.2 %reduce_sum.27 = f32[128,2048]{1,0:T(8,128)S(1)} reduce(f32[8,128,2048]{2,1,0:T(8,128)} %all-to-all-done, f32[]{:T(128)} %constant.4.clone.1), dimensions={0}, to_apply=%region_0.0 | reduce | flops 1835008 | bytes 9437188 | tf_op jit(solution)/shard_map/reduce_sum | solution.py:79
  184.2 2.0 fusion.51
  186.3 2.3 fusion.52
  188.6 16.2 %all-to-all-done.3 = bf16[8,128,1024]{2,1,0:T(8,128)(2,1)S(1)} async-done(((bf16[8,128,1024]{2,1,0:T(8,128)(2,1)}), bf16[8,128,1024]{2,1,0:T(8,128)(2,1)S(1)}, u32[]{:S(2)}, u32[]{:S(2)}) %all-to-all-start.3) | async-done | bytes 2097184 | tf_op jit(solution)/shard_map/all_to_all | solution.py:38
  204.8 2.6 broadcast_in_dim.4
  207.3 7.2 %all-to-all-start.1 = ((bf16[8,128,2048]{2,1,0:T(8,128)(2,1)}), bf16[8,128,2048]{2,1,0:T(8,128)(2,1)}, u32[]{:S(2)}, u32[]{:S(2)}) async-start(bf16[8,128,2048]{2,1,0:T(8,128)(2,1)} %broadcast_in_dim.4), calls=%async_computation.1 | async-start | bytes 8388608 | tf_op jit(solution)/shard_map/all_to_all | solution.py:38
  218.3 1.1 copy-done.17
  219.6 56.5 %all-to-all-done.1 = bf16[8,128,2048]{2,1,0:T(8,128)(2,1)} async-done(((bf16[8,128,2048]{2,1,0:T(8,128)(2,1)}), bf16[8,128,2048]{2,1,0:T(8,128)(2,1)}, u32[]{:S(2)}, u32[]{:S(2)}) %all-to-all-start.1) | async-done | bytes 4194336 | tf_op jit(solution)/shard_map/all_to_all | solution.py:38
  284.6 1.4 fusion.21
  288.2 1.2 fusion.18
  292.6 1.1 copy-done.18
  (102 shorter events, 26.9 us)
Async XLA Ops:
  7.2 2.2 copy-start
  7.2 2.2 copy-start.6
  14.2 10.8 %copy-start.3 = (f32[1,128,4096]{2,1,0:T(8,128)S(1)}, f32[1,128,4096]{2,1,0:T(8,128)}, u32[]{:S(2)}) copy-start(f32[1,128,4096]{2,1,0:T(8,128)} %param.17) | copy-start | bytes 6291460
  16.8 22.6 %all-to-all-start.2 = ((f32[8,64,512]{2,1,0:T(8,128)}), f32[8,64,512]{2,1,0:T(8,128)S(1)}, u32[]{:S(2)}, u32[]{:S(2)}) async-start(f32[8,64,512]{2,1,0:T(8,128)} %fusion.46), calls=%async_computation.2 | async-start | bytes 2097152 | tf_op jit(solution)/shard_map/all_to_all | solution.py:71
  24.9 1.9 copy-start.2
  38.1 8.9 %copy-start.8 = (f32[128,256]{1,0:T(8,128)S(1)}, f32[128,256]{1,0:T(8,128)}, u32[]{:S(2)}) copy-start(f32[128,256]{1,0:T(8,128)} %param.25) | copy-start | bytes 393220
  38.1 8.9 %copy-start.15 = (f32[128,64]{0,1:T(8,128)S(1)}, f32[128,64]{0,1:T(8,128)}, u32[]{:S(2)}) copy-start(f32[128,64]{0,1:T(8,128)} %param.32) | copy-start | bytes 98308
  38.1 9.2 %copy-start.4 = (f32[384,256]{1,0:T(8,128)S(1)}, f32[384,256]{1,0:T(8,128)}, u32[]{:S(2)}) copy-start(f32[384,256]{1,0:T(8,128)} %param.26) | copy-start | bytes 1179652
  39.5 132.0 %all-to-all-start = ((f32[8,128,2048]{2,1,0:T(8,128)}), f32[8,128,2048]{2,1,0:T(8,128)}, u32[]{:S(2)}, u32[]{:S(2)}) async-start(f32[8,128,2048]{2,1,0:T(8,128)} %fusion.9), calls=%async_computation | async-start | bytes 16777216 | tf_op jit(solution)/shard_map/all_to_all | solution.py:79
  47.0 49.0 %all-gather.2.cloned.1.call-start = ((), (), s32[]{:S(2)}) async-start(), calls=%async_computation.4 | async-start | bytes 2228224 | tf_op jit(solution)/shard_map/all_gather | solution.py:73
  47.2 1.4 copy-start.14
  47.6 1.3 copy-start.16
  48.7 49.1 %copy-start.7 = (f32[384,64]{0,1:T(8,128)S(1)}, f32[384,64]{0,1:T(8,128)}, u32[]{:S(2)}) copy-start(f32[384,64]{0,1:T(8,128)} %param.33) | copy-start | bytes 294916
  173.1 31.7 %all-to-all-start.3 = ((bf16[8,128,1024]{2,1,0:T(8,128)(2,1)}), bf16[8,128,1024]{2,1,0:T(8,128)(2,1)S(1)}, u32[]{:S(2)}, u32[]{:S(2)}) async-start(bf16[8,128,1024]{2,1,0:T(8,128)(2,1)} %broadcast_in_dim.5), calls=%async_computation.3 | async-start | bytes 4194304 | tf_op jit(solution)/shard_map/all_to_all | solution.py:38
  184.2 2.0 copy-start.11
  184.2 2.0 copy-start.12
  184.2 2.0 copy-start.13
  207.3 7.2 %copy-start.10 = (f32[128,256]{0,1:T(8,128)S(1)}, f32[128,256]{0,1:T(8,128)}, u32[]{:S(2)}) copy-start(f32[128,256]{0,1:T(8,128)} %get-tuple-element.46) | copy-start | bytes 393220
  207.3 8.0 %copy-start.5 = (f32[384,256]{0,1:T(8,128)S(1)}, f32[384,256]{0,1:T(8,128)}, u32[]{:S(2)}) copy-start(f32[384,256]{0,1:T(8,128)} %get-tuple-element.48) | copy-start | bytes 1179652
  207.3 8.9 %copy-start.9 = (f32[128,256]{0,1:T(8,128)S(1)}, f32[128,256]{0,1:T(8,128)}, u32[]{:S(2)}) copy-start(f32[128,256]{0,1:T(8,128)} %get-tuple-element.142) | copy-start | bytes 393220
  207.3 68.8 %all-to-all-start.1 = ((bf16[8,128,2048]{2,1,0:T(8,128)(2,1)}), bf16[8,128,2048]{2,1,0:T(8,128)(2,1)}, u32[]{:S(2)}, u32[]{:S(2)}) async-start(bf16[8,128,2048]{2,1,0:T(8,128)(2,1)} %broadcast_in_dim.4), calls=%async_computation.1 | async-start | bytes 8388608 | tf_op jit(solution)/shard_map/all_to_all | solution.py:38
  218.3 1.2 copy-start.17
  219.6 66.4 %copy-start.21 = (bf16[128,2048]{1,0:T(8,128)(2,1)}, bf16[128,2048]{1,0:T(8,128)(2,1)S(1)}, u32[]{:S(2)}) copy-start(bf16[128,2048]{1,0:T(8,128)(2,1)S(1)} %constant_dynamic-update-slice_fusion) | copy-start | bytes 1572868
  284.6 4.8 %copy-start.20 = (bf16[128,4096]{1,0:T(8,128)(2,1)}, bf16[128,4096]{1,0:T(8,128)(2,1)S(1)}, u32[]{:S(2)}) copy-start(bf16[128,4096]{1,0:T(8,128)(2,1)S(1)} %fusion.31) | copy-start | bytes 3145732
  288.2 6.1 %copy-start.1 = (f32[1,384,2048]{2,1,0:T(8,128)S(1)}, f32[1,384,2048]{2,1,0:T(8,128)}, u32[]{:S(2)}) copy-start(f32[1,384,2048]{2,1,0:T(8,128)} %param.21) | copy-start | bytes 9437188
  292.6 1.1 copy-start.18
  292.6 1.7 copy-start.19
Sparse Core Ops, SparseCore 0:
  50.1 45.8 all-gather.1

commit v6 on v3

--- a/solution.py
+++ b/solution.py
@@ -81,7 +81,10 @@
         folded = jnp.concatenate([part[k * r_c : (k + 1) * r_c] for k in range(k_c)], axis=1)
         dense = jnp.concatenate([qkv_b[j], one_b[j], three_b[j]], axis=1)
         send.append(jnp.concatenate([dense, folded], axis=0))
-    total = jnp.sum(lax.all_to_all(jnp.stack(send), "rep", 0, 0, tiled=True), axis=0)
+    got = lax.all_to_all(jnp.stack(send), "rep", 0, 0, tiled=True)
+    total = got[0]
+    for g in range(1, n):
+        total = total + got[g]
 
     summed = total[:rows]
     folded = total[rows:]
@@ -101,25 +104,20 @@
     a2, b2, c2 = nesterov(outer_w2, moment_w2, d_down)
 
     dense_w = gather_all(jnp.concatenate([a0, a1, a3], axis=1), "rep", n)
-    q = rows_2 // rows
-    low_w = gather_all(
-        jnp.concatenate([ao] + [a2[k * rows : (k + 1) * rows] for k in range(q)], axis=1), "rep", n
-    )
+    low = lax.all_to_all(
+        jnp.broadcast_to(jnp.concatenate([ao, a2], axis=0)[None], (n, rows + rows_2, w_o)),
+        "rep",
+        0,
+        2,
+        tiled=True,
+    )[0]
     o1 = w_qkv
     o3 = o1 + w_ff
     weights_wqkv = jnp.concatenate([dense_w[j, :, :o1] for j in range(n)], axis=1)
     weights_w1 = jnp.concatenate([dense_w[j, :, o1:o3] for j in range(n)], axis=1)
     weights_w3 = jnp.concatenate([dense_w[j, :, o3:] for j in range(n)], axis=1)
-    weights_wo = jnp.concatenate([low_w[j, :, :w_o] for j in range(n)], axis=1)
-    weights_w2 = jnp.concatenate(
-        [
-            jnp.concatenate(
-                [low_w[j, :, w_o + k * w_2 : w_o + (k + 1) * w_2] for k in range(q)], axis=0
-            )
-            for j in range(n)
-        ],
-        axis=1,
-    )
+    weights_wo = low[:rows]
+    weights_w2 = low[rows:]
     return (
         weights_wqkv,
         weights_w1,

time: 273 us -> 269 us (0.985)
  other arithmetic: 11.5 us -> 6.57 us
  starting transfers between devices: 16.3 us -> 12.4 us
    all_to_all x0 -> x1, waiting for transfers between devices: none -> 13.7 us  [on_device(): lax.all_to_all(jnp.broadcast_to(jnp.concatenate([ao, a2], axis=0)[None],...]
    all_to_all x2 -> x1, waiting for transfers between devices: 66 us -> 54 us  [gather_all(): lax.all_to_all(jnp.broadcast_to(y[None], (n,) + y.shape), axis_name, 0, 0...]
    all_to_all x2 -> x1, starting transfers between devices: 16.3 us -> 6.34 us  [gather_all(): lax.all_to_all(jnp.broadcast_to(y[None], (n,) + y.shape), axis_name, 0, 0...]
    all_to_all x0 -> x1, starting transfers between devices: none -> 6.07 us  [on_device(): lax.all_to_all(jnp.broadcast_to(jnp.concatenate([ao, a2], axis=0)[None],...]
    reduce_sum x1 -> x0, other arithmetic: 4.73 us -> none  [on_device(): jnp.sum(lax.all_to_all(jnp.stack(send), 'rep', 0, 0, tiled=True), axis=0)]
    all_to_all x0 -> x1, local copies, waits for them, and re-layouts: none -> 2.86 us  [on_device(): lax.all_to_all(jnp.broadcast_to(jnp.concatenate([ao, a2], axis=0)[None],...]
    unnamed x69 -> x58, local copies, waits for them, and re-layouts: 34 us -> 32.7 us
  transfers between devices with their start and end apart: 3 -> 3, of which waited for: 2 -> 2; matrix products, arithmetic and copies ran while one was open for 10% -> 11% of each run, Pallas kernels for 0% -> 0%
where the time goes in v6:
time: 269 us; the launch traced here: 268 us
  blocking collectives  114 us (42%)
  waiting for transfers between devices  67.7 us (25%)
  local copies, waits for them, and re-layouts  46.2 us (17%)
  between operations  14.4 us (5%)
  starting transfers between devices  12.4 us (5%)
  other arithmetic  6.57 us (2%)
  matrix products  6.24 us (2%)
    all_to_all x1, blocking collectives, on_device(): got = lax.all_to_all(jnp.stack(send), 'rep', 0, 0, tiled=True)  114 us
    all_to_all x1, waiting for transfers between devices, gather_all(): lax.all_to_all(jnp.broadcast_to(y[None], (n,) + y.shape), axis_name, 0, 0...  54 us
    unnamed x58, local copies, waits for them, and re-layouts  32.7 us
    all_to_all x1, waiting for transfers between devices, on_device(): lax.all_to_all(jnp.broadcast_to(jnp.concatenate([ao, a2], axis=0)[None],...  13.7 us
    all_to_all x1, starting transfers between devices, gather_all(): lax.all_to_all(jnp.broadcast_to(y[None], (n,) + y.shape), axis_name, 0, 0...  6.34 us
    all_to_all x1, starting transfers between devices, on_device(): lax.all_to_all(jnp.broadcast_to(jnp.concatenate([ao, a2], axis=0)[None],...  6.07 us
  transfers between devices with their start and end apart: 3, of which 2 were waited for; matrix products, arithmetic and copies ran while one was open for 11% of the time, Pallas kernels for 0%

profile of v6, /device:TPU:6, one launch (start us, length us, event | category | flops | bytes accessed | tf_op | source)
XLA Modules:
  0.0 267.9 jit_solution(13041841678346261324)
XLA Ops:
  7.2 2.1 fusion.36
  9.4 2.0 fusion
  11.8 1.6 copy-done.2
  15.0 114.3 %all_to_all.25 = f32[8,144,2048]{2,1,0:T(8,128)S(1)} all-to-all(f32[8,144,2048]{2,1,0:T(8,128)S(1)} %fusion.6), channel_id=1, replica_groups=mesh['rep'=8,'shard'=16] {'rep'}, dimensions={0} | all-to-all | bytes 18874368 | tf_op jit(solution)/shard_map/all_to_all | solution.py:84
  131.8 1.3 fusion.94
  133.1 2.6 broadcast_in_dim.4
  135.6 6.3 %all-to-all-start.1 = ((bf16[8,128,2048]{2,1,0:T(8,128)(2,1)}), bf16[8,128,2048]{2,1,0:T(8,128)(2,1)}, u32[]{:S(2)}, u32[]{:S(2)}) async-start(bf16[8,128,2048]{2,1,0:T(8,128)(2,1)} %broadcast_in_dim.4), calls=%async_computation.1 | async-start | bytes 8388608 | tf_op jit(solution)/shard_map/all_to_all | solution.py:38
  143.6 54.0 %all-to-all-done.1 = bf16[8,128,2048]{2,1,0:T(8,128)(2,1)} async-done(((bf16[8,128,2048]{2,1,0:T(8,128)(2,1)}), bf16[8,128,2048]{2,1,0:T(8,128)(2,1)}, u32[]{:S(2)}, u32[]{:S(2)}) %all-to-all-start.1) | async-done | bytes 4194336 | tf_op jit(solution)/shard_map/all_to_all | solution.py:38
  197.6 1.6 fusion.64
  199.2 1.6 fusion.63
  200.8 1.6 fusion.62
  202.3 1.6 fusion.61
  203.9 1.6 fusion.60
  205.5 1.6 fusion.59
  207.1 1.6 fusion.58
  208.6 1.8 fusion.48
  210.4 1.8 reduce_sum.9
  214.1 1.5 broadcast_in_dim.5
  215.7 6.1 %all-to-all-start.2 = ((bf16[8,512,256]{2,1,0:T(8,128)(2,1)}), bf16[8,512,256]{2,1,0:T(8,128)(2,1)}, u32[]{:S(2)}, u32[]{:S(2)}) async-start(bf16[8,512,256]{2,1,0:T(8,128)(2,1)} %broadcast_in_dim.5), calls=%async_computation.2 | async-start | bytes 4194304 | tf_op jit(solution)/shard_map/all_to_all | solution.py:107
  221.7 1.6 fusion.57
  223.3 1.7 fusion.47
  225.0 1.7 fusion.46
  226.8 1.7 fusion.45
  228.5 1.7 fusion.44
  230.2 1.7 fusion.43
  232.0 1.7 fusion.42
  233.7 1.7 fusion.41
  237.4 13.7 %all-to-all-done.2 = bf16[8,512,256]{2,1,0:T(8,128)(2,1)} async-done(((bf16[8,512,256]{2,1,0:T(8,128)(2,1)}), bf16[8,512,256]{2,1,0:T(8,128)(2,1)}, u32[]{:S(2)}, u32[]{:S(2)}) %all-to-all-start.2) | async-done | bytes 2097184 | tf_op jit(solution)/shard_map/all_to_all | solution.py:107
  251.1 2.9 %copy.48 = bf16[8,512,256]{1,2,0:T(8,128)(2,1)S(1)} copy(bf16[8,512,256]{2,1,0:T(8,128)(2,1)} %all-to-all-done.2) | data formatting | bytes 4194304 | tf_op jit(solution)/shard_map/all_to_all | solution.py:107
  254.0 1.3 slice.607
  256.2 2.7 %copy.50 = bf16[384,2048]{1,0:T(8,128)(2,1)} copy(bf16[384,2048]{0,1:T(8,128)(2,1)} %bitcast.170) | data formatting | bytes 3145728
  259.0 2.0 copy.49
  (73 shorter events, 10.8 us)
Async XLA Ops:
  7.2 2.2 copy-start
  7.2 2.2 copy-start.6
  9.3 2.2 copy-start.4
  9.4 2.4 copy-start.3
  11.5 2.0 copy-start.2
  129.3 1.0 copy-start.14
  129.3 1.0 copy-start.15
  129.3 1.9 copy-start.11
  130.3 1.0 copy-start.8
  130.3 1.3 copy-start.9
  130.3 1.4 copy-start.10
  135.6 6.4 %copy-start.7 = (f32[128,256]{1,0:T(8,128)S(1)}, f32[128,256]{1,0:T(8,128)}, u32[]{:S(2)}) copy-start(f32[128,256]{1,0:T(8,128)} %param.25) | copy-start | bytes 393220
  135.6 6.4 %copy-start.13 = (f32[128,64]{0,1:T(8,128)S(1)}, f32[128,64]{0,1:T(8,128)}, u32[]{:S(2)}) copy-start(f32[128,64]{0,1:T(8,128)} %param.32) | copy-start | bytes 98308
  135.6 6.6 %copy-start.5 = (f32[384,256]{1,0:T(8,128)S(1)}, f32[384,256]{1,0:T(8,128)}, u32[]{:S(2)}) copy-start(f32[384,256]{1,0:T(8,128)} %param.26) | copy-start | bytes 1179652
  135.6 62.0 %all-to-all-start.1 = ((bf16[8,128,2048]{2,1,0:T(8,128)(2,1)}), bf16[8,128,2048]{2,1,0:T(8,128)(2,1)}, u32[]{:S(2)}, u32[]{:S(2)}) async-start(bf16[8,128,2048]{2,1,0:T(8,128)(2,1)} %broadcast_in_dim.4), calls=%async_computation.1 | async-start | bytes 8388608 | tf_op jit(solution)/shard_map/all_to_all | solution.py:38
  142.0 1.5 copy-start.12
  142.0 68.4 %all-gather.2.cloned.1.call-start = ((), (), s32[]{:S(2)}) async-start(), calls=%async_computation.3 | async-start | bytes 2228224 | tf_op jit(solution)/shard_map/all_gather | solution.py:93
  210.4 1.8 copy-start.16
  215.7 7.6 %copy-start.17 = (bf16[128,6144]{1,0:T(8,128)(2,1)S(1)}, bf16[128,6144]{1,0:T(8,128)(2,1)}, u32[]{:S(2)}) copy-start(bf16[128,6144]{1,0:T(8,128)(2,1)} %get-tuple-element.88) | copy-start | bytes 4718596
  215.7 35.4 %all-to-all-start.2 = ((bf16[8,512,256]{2,1,0:T(8,128)(2,1)}), bf16[8,512,256]{2,1,0:T(8,128)(2,1)}, u32[]{:S(2)}, u32[]{:S(2)}) async-start(bf16[8,512,256]{2,1,0:T(8,128)(2,1)} %broadcast_in_dim.5), calls=%async_computation.2 | async-start | bytes 4194304 | tf_op jit(solution)/shard_map/all_to_all | solution.py:107
  235.4 2.0 copy-start.18
  256.2 4.8 %copy-start.1 = (f32[1,384,2048]{2,1,0:T(8,128)S(1)}, f32[1,384,2048]{2,1,0:T(8,128)}, u32[]{:S(2)}) copy-start(f32[1,384,2048]{2,1,0:T(8,128)} %param.21) | copy-start | bytes 9437188
Sparse Core Ops, SparseCore 0:
  145.0 58.7 all-gather.1

commit v7 on v6

--- a/solution.py
+++ b/solution.py
@@ -32,6 +32,11 @@
 def owner_blocks(a, n):
     w = a.shape[1] // n
     return [a[:, j * w : (j + 1) * w] for j in range(n)]
+
+
+def from_owners(g):
+    n, r, w = g.shape
+    return g.transpose(1, 0, 2).reshape(r, n * w)
 
 
 def gather_all(y, axis_name, n):
@@ -104,20 +109,14 @@
     a2, b2, c2 = nesterov(outer_w2, moment_w2, d_down)
 
     dense_w = gather_all(jnp.concatenate([a0, a1, a3], axis=1), "rep", n)
-    low = lax.all_to_all(
-        jnp.broadcast_to(jnp.concatenate([ao, a2], axis=0)[None], (n, rows + rows_2, w_o)),
-        "rep",
-        0,
-        2,
-        tiled=True,
-    )[0]
+    low_w = gather_all(jnp.concatenate([ao, a2], axis=0), "rep", n)
     o1 = w_qkv
     o3 = o1 + w_ff
-    weights_wqkv = jnp.concatenate([dense_w[j, :, :o1] for j in range(n)], axis=1)
-    weights_w1 = jnp.concatenate([dense_w[j, :, o1:o3] for j in range(n)], axis=1)
-    weights_w3 = jnp.concatenate([dense_w[j, :, o3:] for j in range(n)], axis=1)
-    weights_wo = low[:rows]
-    weights_w2 = low[rows:]
+    weights_wqkv = from_owners(dense_w[:, :, :o1])
+    weights_w1 = from_owners(dense_w[:, :, o1:o3])
+    weights_w3 = from_owners(dense_w[:, :, o3:])
+    weights_wo = from_owners(low_w[:, :rows])
+    weights_w2 = from_owners(low_w[:, rows:])
     return (
         weights_wqkv,
         weights_w1,

time: 269 us -> 310 us (1.15)
  waiting for transfers between devices: 67.7 us -> 201 us
  blocking collectives: 114 us -> 0 us
  other arithmetic: 6.57 us -> 20.5 us
  starting transfers between devices: 12.4 us -> 24.5 us
  local copies, waits for them, and re-layouts: 46.2 us -> 41.5 us
    all_to_all x1, waiting for transfers between devices: 13.7 us -> 139 us  [on_device(): got = lax.all_to_all(jnp.stack(send), 'rep', 0, 0, tiled=True)]
    all_to_all x1 -> x0, blocking collectives: 114 us -> none  [on_device(): got = lax.all_to_all(jnp.stack(send), 'rep', 0, 0, tiled=True)]
    all_gather x1, waiting for transfers between devices: 0.01 us -> 53.3 us  [on_device(): lax.all_gather(own - part / n, 'shard', axis=0, tiled=False)]
    all_to_all x1 -> x2, waiting for transfers between devices: 54 us -> 8.56 us  [gather_all(): lax.all_to_all(jnp.broadcast_to(y[None], (n,) + y.shape), axis_name, 0, 0...]
    all_to_all x1 -> x2, starting transfers between devices: 6.34 us -> 16.3 us  [gather_all(): lax.all_to_all(jnp.broadcast_to(y[None], (n,) + y.shape), axis_name, 0, 0...]
    unnamed x7, other arithmetic: 0.79 us -> 8.03 us
    slice x2 -> x4, local copies, waits for them, and re-layouts: 2.25 us -> 8.47 us  [the longest x1 3.83 us: on_device(): weights_w3 = from_owners(dense_w[:, :, o3:])]
    unnamed x58 -> x50, local copies, waits for them, and re-layouts: 32.7 us -> 27.8 us
  transfers between devices with their start and end apart: 3 -> 4, of which waited for: 2 -> 3; matrix products, arithmetic and copies ran while one was open for 11% -> 11% of each run, Pallas kernels for 0% -> 0%
where the time goes in v7:
time: 310 us; the launch traced here: 309 us
  waiting for transfers between devices  201 us (65%)
  local copies, waits for them, and re-layouts  41.5 us (13%)
  starting transfers between devices  24.5 us (8%)
  other arithmetic  20.5 us (7%)
  between operations  14.4 us (5%)
  matrix products  6.97 us (2%)
    all_to_all x1, waiting for transfers between devices, on_device(): got = lax.all_to_all(jnp.stack(send), 'rep', 0, 0, tiled=True)  139 us
    all_gather x1, waiting for transfers between devices, on_device(): lax.all_gather(own - part / n, 'shard', axis=0, tiled=False)  53.3 us
    unnamed x50, local copies, waits for them, and re-layouts  27.8 us
    all_to_all x2, starting transfers between devices, gather_all(): lax.all_to_all(jnp.broadcast_to(y[None], (n,) + y.shape), axis_name, 0, 0...  16.3 us
    all_to_all x2, waiting for transfers between devices, gather_all(): lax.all_to_all(jnp.broadcast_to(y[None], (n,) + y.shape), axis_name, 0, 0...  8.56 us
    all_to_all x1, starting transfers between devices, on_device(): got = lax.all_to_all(jnp.stack(send), 'rep', 0, 0, tiled=True)  8.22 us
    unnamed x7, other arithmetic  8.03 us
  transfers between devices with their start and end apart: 4, of which 3 were waited for; matrix products, arithmetic and copies ran while one was open for 11% of the time, Pallas kernels for 0%

profile of v7, /device:TPU:6, one launch (start us, length us, event | category | flops | bytes accessed | tf_op | source)
XLA Modules:
  0.0 309.0 jit_solution(14447456188764396943)
XLA Ops:
  7.2 2.1 fusion.36
  9.4 2.0 fusion
  11.8 1.6 copy-done.3
  16.5 1.2 fusion.26
  21.1 1.2 fusion.10
  23.4 8.2 %all-to-all-start = ((f32[8,144,2048]{2,1,0:T(8,128)}), f32[8,144,2048]{2,1,0:T(8,128)}, u32[]{:S(2)}, u32[]{:S(2)}) async-start(f32[8,144,2048]{2,1,0:T(8,128)} %fusion.6), calls=%async_computation | async-start | bytes 18874368 | tf_op jit(solution)/shard_map/all_to_all | solution.py:89
  32.2 139.2 %all-to-all-done = f32[8,144,2048]{2,1,0:T(8,128)} async-done(((f32[8,144,2048]{2,1,0:T(8,128)}), f32[8,144,2048]{2,1,0:T(8,128)}, u32[]{:S(2)}, u32[]{:S(2)}) %all-to-all-start) | async-done | bytes 9437216 | tf_op jit(solution)/shard_map/all_to_all | solution.py:89
  171.4 4.7 %fusion.2 = f32[144,2048]{1,0:T(8,128)S(1)} fusion(f32[8,144,2048]{2,1,0:T(8,128)} %all-to-all-done), kind=kLoop, calls=%fused_computation.4 | loop fusion | flops 2064384 | bytes 10616832 | tf_op jit(solution)/shard_map/add | solution.py:92
  176.9 1.8 fusion.69
  178.8 2.3 fusion.70
  181.1 2.6 broadcast_in_dim.4
  183.6 7.0 %all-to-all-start.1 = ((bf16[8,128,2048]{2,1,0:T(8,128)(2,1)}), bf16[8,128,2048]{2,1,0:T(8,128)(2,1)}, u32[]{:S(2)}, u32[]{:S(2)}) async-start(bf16[8,128,2048]{2,1,0:T(8,128)(2,1)} %broadcast_in_dim.4), calls=%async_computation.1 | async-start | bytes 8388608 | tf_op jit(solution)/shard_map/all_to_all | solution.py:43
  191.0 53.3 %all-gather.2.cloned.1.call-done = f32[16,64,512]{2,1,0:T(8,128)} async-done(((f32[1,64,512]{2,1,0:T(8,128)}), f32[16,64,512]{2,1,0:T(8,128)}) %all-gather.2.cloned.1.call-update) | async-done | bytes 2097168 | tf_op jit(solution)/shard_map/all_gather | solution.py:98
  244.3 1.8 reduce_sum.9
  247.3 1.3 fusion.68
  248.8 1.5 broadcast_in_dim.5
  250.3 9.2 %all-to-all-start.2 = ((bf16[8,512,256]{2,1,0:T(8,128)(2,1)}), bf16[8,512,256]{2,1,0:T(8,128)(2,1)S(1)}, u32[]{:S(2)}, u32[]{:S(2)}) async-start(bf16[8,512,256]{2,1,0:T(8,128)(2,1)} %broadcast_in_dim.5), calls=%async_computation.2 | async-start | bytes 4194304 | tf_op jit(solution)/shard_map/all_to_all | solution.py:43
  259.5 3.8 %fusion.72 = (bf16[8,128,768]{2,1,0:T(8,128)(2,1)}, bf16[8,128,768]{2,1,0:T(8,128)(2,1)}) fusion(bf16[8,128,2048]{2,1,0:T(8,128)(2,1)} %all-to-all-done.1), kind=kLoop, calls=%fused_computation.162 | loop fusion | bytes 6291456 | tf_op jit(solution)/shard_map/slice | solution.py:117
  263.3 2.6 copy.61
  266.0 2.6 copy.54
  268.5 2.6 copy.62
  271.1 2.6 copy.55
  273.7 1.3 slice.484
  275.0 1.3 copy.60
  276.3 2.3 copy.53
  280.5 8.6 %all-to-all-done.2 = bf16[8,512,256]{2,1,0:T(8,128)(2,1)S(1)} async-done(((bf16[8,512,256]{2,1,0:T(8,128)(2,1)}), bf16[8,512,256]{2,1,0:T(8,128)(2,1)S(1)}, u32[]{:S(2)}, u32[]{:S(2)}) %all-to-all-start.2) | async-done | bytes 2097184 | tf_op jit(solution)/shard_map/all_to_all | solution.py:43
  289.0 1.3 slice.494
  290.9 2.6 copy.64
  293.4 2.6 copy.57
  296.0 2.0 slice.493
  298.0 2.0 copy.63
  300.1 2.0 copy.56
  (65 shorter events, 13.3 us)
Async XLA Ops:
  7.2 2.2 copy-start
  7.2 2.2 copy-start.8
  9.3 2.2 copy-start.5
  9.4 2.4 copy-start.4
  11.5 2.0 copy-start.3
  23.4 8.2 %copy-start.10 = (f32[128,256]{1,0:T(8,128)S(1)}, f32[128,256]{1,0:T(8,128)}, u32[]{:S(2)}) copy-start(f32[128,256]{1,0:T(8,128)} %param.25) | copy-start | bytes 393220
  23.4 8.2 %copy-start.15 = (f32[128,64]{0,1:T(8,128)S(1)}, f32[128,64]{0,1:T(8,128)}, u32[]{:S(2)}) copy-start(f32[128,64]{0,1:T(8,128)} %param.32) | copy-start | bytes 98308
  23.4 8.5 %copy-start.6 = (f32[384,256]{1,0:T(8,128)S(1)}, f32[384,256]{1,0:T(8,128)}, u32[]{:S(2)}) copy-start(f32[384,256]{1,0:T(8,128)} %param.26) | copy-start | bytes 1179652
  23.4 148.0 %all-to-all-start = ((f32[8,144,2048]{2,1,0:T(8,128)}), f32[8,144,2048]{2,1,0:T(8,128)}, u32[]{:S(2)}, u32[]{:S(2)}) async-start(f32[8,144,2048]{2,1,0:T(8,128)} %fusion.6), calls=%async_computation | async-start | bytes 18874368 | tf_op jit(solution)/shard_map/all_to_all | solution.py:89
  31.6 212.7 %all-gather.2.cloned.1.call-start = ((), (), s32[]{:S(2)}) async-start(), calls=%async_computation.3 | async-start | bytes 2228224 | tf_op jit(solution)/shard_map/all_gather | solution.py:98
  32.2 144.7 %copy-start.16 = (f32[128,512]{1,0:T(8,128)S(1)}, f32[128,512]{1,0:T(8,128)}, u32[]{:S(2)}) copy-start(f32[128,512]{1,0:T(8,128)} %param.22) | copy-start | bytes 786436
  176.1 2.6 copy-start.11
  176.2 2.6 copy-start.12
  176.2 2.6 copy-start.13
  183.6 7.2 %copy-start.14 = (f32[384,256]{1,0:T(8,128)S(1)}, f32[384,256]{1,0:T(8,128)}, u32[]{:S(2)}) copy-start(f32[384,256]{1,0:T(8,128)} %param.31) | copy-start | bytes 1179652
  183.6 65.2 %all-to-all-start.1 = ((bf16[8,128,2048]{2,1,0:T(8,128)(2,1)}), bf16[8,128,2048]{2,1,0:T(8,128)(2,1)}, u32[]{:S(2)}, u32[]{:S(2)}) async-start(bf16[8,128,2048]{2,1,0:T(8,128)(2,1)} %broadcast_in_dim.4), calls=%async_computation.1 | async-start | bytes 8388608 | tf_op jit(solution)/shard_map/all_to_all | solution.py:43
  191.0 55.1 %copy-start.17 = (f32[128,256]{1,0:T(8,128)S(1)}, f32[128,256]{1,0:T(8,128)}, u32[]{:S(2)}) copy-start(f32[128,256]{1,0:T(8,128)} %param.30) | copy-start | bytes 393220
  191.0 56.2 %copy-start.9 = (f32[384,64]{0,1:T(8,128)S(1)}, f32[384,64]{0,1:T(8,128)}, u32[]{:S(2)}) copy-start(f32[384,64]{0,1:T(8,128)} %param.33) | copy-start | bytes 294916
  250.3 38.7 %all-to-all-start.2 = ((bf16[8,512,256]{2,1,0:T(8,128)(2,1)}), bf16[8,512,256]{2,1,0:T(8,128)(2,1)S(1)}, u32[]{:S(2)}, u32[]{:S(2)}) async-start(bf16[8,512,256]{2,1,0:T(8,128)(2,1)} %broadcast_in_dim.5), calls=%async_computation.2 | async-start | bytes 4194304 | tf_op jit(solution)/shard_map/all_to_all | solution.py:43
  276.3 2.3 copy-start.7
  289.0 1.8 copy-start.2
  296.0 6.1 %copy-start.1 = (f32[1,384,2048]{2,1,0:T(8,128)S(1)}, f32[1,384,2048]{2,1,0:T(8,128)}, u32[]{:S(2)}) copy-start(f32[1,384,2048]{2,1,0:T(8,128)} %param.21) | copy-start | bytes 9437188
Sparse Core Ops, SparseCore 0:
  177.0 67.2 all-gather.1

commit v8 on v3

--- a/solution.py
+++ b/solution.py
@@ -81,7 +81,10 @@
         folded = jnp.concatenate([part[k * r_c : (k + 1) * r_c] for k in range(k_c)], axis=1)
         dense = jnp.concatenate([qkv_b[j], one_b[j], three_b[j]], axis=1)
         send.append(jnp.concatenate([dense, folded], axis=0))
-    total = jnp.sum(lax.all_to_all(jnp.stack(send), "rep", 0, 0, tiled=True), axis=0)
+    got = lax.all_to_all(jnp.stack(send), "rep", 0, 0, tiled=True)
+    total = got[0]
+    for g in range(1, n):
+        total = total + got[g]
 
     summed = total[:rows]
     folded = total[rows:]

time: 273 us -> 268 us (0.982)
  other arithmetic: 11.5 us -> 6.66 us
    reduce_sum x1 -> x0, other arithmetic: 4.73 us -> none  [on_device(): jnp.sum(lax.all_to_all(jnp.stack(send), 'rep', 0, 0, tiled=True), axis=0)]
    unnamed x69 -> x71, local copies, waits for them, and re-layouts: 34 us -> 34.1 us
where the time goes in v8:
time: 268 us; the launch traced here: 267 us
  blocking collectives  114 us (43%)
  waiting for transfers between devices  65.9 us (25%)
  local copies, waits for them, and re-layouts  43.8 us (16%)
  starting transfers between devices  16.4 us (6%)
  between operations  14.5 us (5%)
  other arithmetic  6.66 us (2%)
  matrix products  5.6 us (2%)
    all_to_all x1, blocking collectives, on_device(): got = lax.all_to_all(jnp.stack(send), 'rep', 0, 0, tiled=True)  114 us
    all_to_all x2, waiting for transfers between devices, gather_all(): lax.all_to_all(jnp.broadcast_to(y[None], (n,) + y.shape), axis_name, 0, 0...  65.9 us
    unnamed x71, local copies, waits for them, and re-layouts  34.1 us
    all_to_all x2, starting transfers between devices, gather_all(): lax.all_to_all(jnp.broadcast_to(y[None], (n,) + y.shape), axis_name, 0, 0...  16.4 us
  transfers between devices with their start and end apart: 3, of which 2 were waited for; matrix products, arithmetic and copies ran while one was open for 10% of the time, Pallas kernels for 0%

profile of v8, /device:TPU:6, one launch (start us, length us, event | category | flops | bytes accessed | tf_op | source)
XLA Modules:
  0.0 267.2 jit_solution(1608053463430546735)
XLA Ops:
  7.2 2.1 fusion.36
  9.4 2.0 fusion
  11.8 1.6 copy-done.3
  15.2 114.3 %all_to_all.15 = f32[8,144,2048]{2,1,0:T(8,128)S(1)} all-to-all(f32[8,144,2048]{2,1,0:T(8,128)S(1)} %fusion.6), channel_id=1, replica_groups=mesh['rep'=8,'shard'=16] {'rep'}, dimensions={0} | all-to-all | bytes 18874368 | tf_op jit(solution)/shard_map/all_to_all | solution.py:84
  129.5 0.9 fusion.2
  132.0 1.3 fusion.94
  133.3 2.6 broadcast_in_dim.4
  135.9 6.3 %all-to-all-start.1 = ((bf16[8,128,2048]{2,1,0:T(8,128)(2,1)}), bf16[8,128,2048]{2,1,0:T(8,128)(2,1)}, u32[]{:S(2)}, u32[]{:S(2)}) async-start(bf16[8,128,2048]{2,1,0:T(8,128)(2,1)} %broadcast_in_dim.4), calls=%async_computation.1 | async-start | bytes 8388608 | tf_op jit(solution)/shard_map/all_to_all | solution.py:38
  144.1 53.8 %all-to-all-done.1 = bf16[8,128,2048]{2,1,0:T(8,128)(2,1)} async-done(((bf16[8,128,2048]{2,1,0:T(8,128)(2,1)}), bf16[8,128,2048]{2,1,0:T(8,128)(2,1)}, u32[]{:S(2)}, u32[]{:S(2)}) %all-to-all-start.1) | async-done | bytes 4194336 | tf_op jit(solution)/shard_map/all_to_all | solution.py:38
  197.9 0.9 fusion.64
  198.8 0.9 fusion.63
  199.7 0.9 fusion.62
  200.6 0.9 fusion.61
  201.5 0.9 fusion.60
  202.5 0.9 fusion.59
  203.4 0.9 fusion.58
  204.3 2.2 fusion.48
  206.5 1.8 reduce_sum.9
  209.5 1.6 broadcast_in_dim.5
  211.1 10.1 %all-to-all-start.2 = ((bf16[8,128,1024]{2,1,0:T(8,128)(2,1)}), bf16[8,128,1024]{2,1,0:T(8,128)(2,1)S(1)}, u32[]{:S(2)}, u32[]{:S(2)}) async-start(bf16[8,128,1024]{2,1,0:T(8,128)(2,1)} %broadcast_in_dim.5), calls=%async_computation.2 | async-start | bytes 4194304 | tf_op jit(solution)/shard_map/all_to_all | solution.py:38
  221.2 1.6 fusion.57
  222.7 1.8 fusion.47
  224.5 1.8 fusion.46
  226.3 1.8 fusion.45
  228.1 1.8 fusion.44
  229.9 1.8 fusion.43
  231.7 1.8 fusion.42
  233.5 1.8 fusion.41
  238.6 12.1 %all-to-all-done.2 = bf16[8,128,1024]{2,1,0:T(8,128)(2,1)S(1)} async-done(((bf16[8,128,1024]{2,1,0:T(8,128)(2,1)}), bf16[8,128,1024]{2,1,0:T(8,128)(2,1)S(1)}, u32[]{:S(2)}, u32[]{:S(2)}) %all-to-all-start.2) | async-done | bytes 2097184 | tf_op jit(solution)/shard_map/all_to_all | solution.py:38
  250.9 1.1 copy-done.2
  252.2 1.1 constant_dynamic-update-slice_fusion.7
  253.3 1.1 constant_dynamic-update-slice_fusion.6
  (94 shorter events, 16.2 us)
Async XLA Ops:
  7.2 2.2 copy-start
  7.2 2.2 copy-start.7
  9.3 2.2 copy-start.5
  9.4 2.4 copy-start.4
  11.5 2.0 copy-start.3
  129.5 1.0 copy-start.15
  129.5 1.0 copy-start.16
  129.5 1.9 copy-start.12
  130.5 1.0 copy-start.9
  130.5 1.3 copy-start.10
  130.5 1.4 copy-start.11
  135.8 6.4 %copy-start.8 = (f32[128,256]{1,0:T(8,128)S(1)}, f32[128,256]{1,0:T(8,128)}, u32[]{:S(2)}) copy-start(f32[128,256]{1,0:T(8,128)} %param.25) | copy-start | bytes 393220
  135.8 6.4 %copy-start.14 = (f32[128,64]{0,1:T(8,128)S(1)}, f32[128,64]{0,1:T(8,128)}, u32[]{:S(2)}) copy-start(f32[128,64]{0,1:T(8,128)} %param.32) | copy-start | bytes 98308
  135.9 6.6 %copy-start.6 = (f32[384,256]{1,0:T(8,128)S(1)}, f32[384,256]{1,0:T(8,128)}, u32[]{:S(2)}) copy-start(f32[384,256]{1,0:T(8,128)} %param.26) | copy-start | bytes 1179652
  135.9 62.0 %all-to-all-start.1 = ((bf16[8,128,2048]{2,1,0:T(8,128)(2,1)}), bf16[8,128,2048]{2,1,0:T(8,128)(2,1)}, u32[]{:S(2)}, u32[]{:S(2)}) async-start(bf16[8,128,2048]{2,1,0:T(8,128)(2,1)} %broadcast_in_dim.4), calls=%async_computation.1 | async-start | bytes 8388608 | tf_op jit(solution)/shard_map/all_to_all | solution.py:38
  142.2 64.3 %all-gather.2.cloned.1.call-start = ((), (), s32[]{:S(2)}) async-start(), calls=%async_computation.3 | async-start | bytes 2228224 | tf_op jit(solution)/shard_map/all_gather | solution.py:93
  142.4 1.4 copy-start.13
  142.8 1.2 copy-start.17
  204.3 2.2 copy-start.19
  211.1 39.6 %all-to-all-start.2 = ((bf16[8,128,1024]{2,1,0:T(8,128)(2,1)}), bf16[8,128,1024]{2,1,0:T(8,128)(2,1)S(1)}, u32[]{:S(2)}, u32[]{:S(2)}) async-start(bf16[8,128,1024]{2,1,0:T(8,128)(2,1)} %broadcast_in_dim.5), calls=%async_computation.2 | async-start | bytes 4194304 | tf_op jit(solution)/shard_map/all_to_all | solution.py:38
  250.7 1.3 copy-start.2
  252.1 8.3 %copy-start.1 = (f32[1,384,2048]{2,1,0:T(8,128)S(1)}, f32[1,384,2048]{2,1,0:T(8,128)}, u32[]{:S(2)}) copy-start(f32[1,384,2048]{2,1,0:T(8,128)} %param.21) | copy-start | bytes 9437188
  252.2 7.4 %copy-start.18 = (bf16[384,2048]{1,0:T(8,128)(2,1)}, bf16[384,2048]{1,0:T(8,128)(2,1)S(1)}, u32[]{:S(2)}) copy-start(bf16[384,2048]{1,0:T(8,128)(2,1)S(1)} %maximum_dynamic-update-slice_fusion) | copy-start | bytes 4718596
  259.6 0.8 copy-start.20
Sparse Core Ops, SparseCore 0:
  145.3 58.7 all-gather.1
